TPU v7x, 512 devices: a whole 4x8x8 slice. The times are simulated.
512 devices in a mesh: shard: 128 (over z, y, core), tensor: 4 (over x).
Axes of the slice: x: 4, y: 8, z: 8, core: 2. Of those that a mesh axis runs over, the one named last changes fastest.
Arguments:
- grad_query: bfloat16 [4, 2048, 2048], P(None, 'shard', 'tensor'), may hold values from -300 to 300, as said below
- grad_key: bfloat16 [4, 2048, 2048], P(None, 'shard', 'tensor'), may hold values from -300 to 300
- grad_value: bfloat16 [4, 2048, 2048], P(None, 'shard', 'tensor'), may hold values from -300 to 300
- grad_output: bfloat16 [4, 2048, 2048], P(None, 'shard', 'tensor'), may hold values from -300 to 300
- grad_gate: bfloat16 [4, 2048, 5120], P(None, 'shard', 'tensor'), may hold values from -300 to 300
- grad_linear: bfloat16 [4, 2048, 5120], P(None, 'shard', 'tensor'), may hold values from -300 to 300
- grad_down: bfloat16 [4, 2048, 5120], P(None, 'shard', 'tensor'), may hold values from -300 to 300
- grad_norms: bfloat16 [4, 4, 2, 2048], P(None, 'tensor', None, 'shard'), may hold values from -24 to 24
- master_flat: float32 [128, 4, 94208], P('shard', 'tensor'), may hold values from -4 to 4
- first_moment: float32 [128, 4, 94208], P('shard', 'tensor'), may hold values from -3 to 3
- second_moment: float32 [128, 4, 94208], P('shard', 'tensor'), may hold values from 0.05 to 1
- gain_master: float32 [2, 2048], P(None, 'shard'), may hold values from 0.5 to 1.5
- gain_first: float32 [2, 2048], P(None, 'shard'), may hold values from -3 to 3
- gain_second: float32 [2, 2048], P(None, 'shard'), may hold values from 0.05 to 1
Outputs:
- new_master: float32 [128, 4, 94208], P('shard', 'tensor')
- new_first: float32 [128, 4, 94208], P('shard', 'tensor')
- new_second: float32 [128, 4, 94208], P('shard', 'tensor')
- new_gains: float32 [2, 2048], P(None, 'shard')
- new_gain_first: float32 [2, 2048], P(None, 'shard')
- new_gain_second: float32 [2, 2048], P(None, 'shard')
- copy_query: bfloat16 [2048, 2048], P('shard', 'tensor')
- copy_key: bfloat16 [2048, 2048], P('shard', 'tensor')
- copy_value: bfloat16 [2048, 2048], P('shard', 'tensor')
- copy_output: bfloat16 [2048, 2048], P('shard', 'tensor')
- copy_gate: bfloat16 [2048, 5120], P('shard', 'tensor')
- copy_linear: bfloat16 [2048, 5120], P('shard', 'tensor')
- copy_down: bfloat16 [2048, 5120], P('shard', 'tensor')
- copy_gains: bfloat16 [2, 2048], P(None, 'shard')
- grad_rms: float32 [], replicated
Inputs may be any that keep to these rules, and one draw needn't show every extreme that they name: `grad_query`: grad_rms is above 0.5 in every draw, so the clip factor is below one.
All inputs are finite; a program needn't handle non-finite values.
Results may differ from a plain program's by a relative error of at most 0.00045.
Values may be sent and summed in bfloat16 or wider, within the bound.
No kernel may reach another device: no remote copies, remote signals or barrier semaphores. Data moves between devices by JAX's collectives and lax.ppermute only.
A program may use at most 64 MiB of HBM per device.

v0:
```python
import jax
import jax.numpy as jnp
from jax import lax
from jax.sharding import PartitionSpec as P

MB = 4
STEP = 20
COUNT = 48238592


BETA1 = 0.9
BETA2 = 0.95
EPSILON = 1e-08
LRATE = 0.2
WDECAY = 2.5
CLIP_RMS = 0.5


def adamw(weight, gradient, moment_one, moment_two, decay_rate, factor):
    clipped = gradient * factor
    moment_one_new = BETA1 * moment_one + (1.0 - BETA1) * clipped
    moment_two_new = BETA2 * moment_two + (1.0 - BETA2) * clipped * clipped
    update = (
        moment_one_new
        / (1.0 - BETA1**STEP)
        / (jnp.sqrt(moment_two_new / (1.0 - BETA2**STEP)) + EPSILON)
    )
    return (weight - LRATE * (update + decay_rate * weight), moment_one_new, moment_two_new)


def mean_block(matrix):
    return jnp.sum(matrix.astype(jnp.float32), axis=0) * (1.0 / MB)


def by_destination(group_means, shard_count):
    rows = group_means[0].shape[0]
    sections = [
        matrix.reshape(rows, shard_count, matrix.shape[-1] // shard_count) for matrix in group_means
    ]
    joined = jnp.concatenate(sections, axis=-1)
    return jnp.transpose(joined, (1, 0, 2)).reshape(shard_count, -1)


def shards(
    grad_query,
    grad_key,
    grad_value,
    grad_output,
    grad_gate,
    grad_linear,
    grad_down,
    grad_norms,
    master_flat,
    first_moment,
    second_moment,
    gain_master,
    gain_first,
    gain_second,
):
    blocks = [grad_query, grad_key, grad_value, grad_output, grad_gate, grad_linear, grad_down]
    shard_count = lax.axis_size("shard")
    rows = grad_query.shape[1]
    group_widths = [matrix.shape[2] // shard_count for matrix in blocks]
    flat_width = sum(group_widths)

    group_means = [mean_block(matrix) for matrix in blocks]
    block_square = jnp.sum(group_means[0] * group_means[0])
    for averaged in group_means[1:]:
        block_square = block_square + jnp.sum(averaged * averaged)

    gain_local = jnp.sum(grad_norms.astype(jnp.float32), axis=(0, 1))
    gain_size = gain_local.size
    summed = lax.psum(jnp.concatenate([gain_local.reshape(-1), block_square.reshape(1)]), "tensor")
    gain_grad = summed[:gain_size].reshape(gain_local.shape) * (1.0 / MB)
    shard_square = summed[gain_size] + jnp.sum(gain_grad * gain_grad)

    payload = by_destination(group_means, shard_count)
    payload = jnp.concatenate(
        [payload, jnp.broadcast_to(shard_square, (shard_count, 1))], axis=1
    )
    received = lax.all_to_all(payload, "shard", split_axis=0, concat_axis=0, tiled=True)
    square_total = jnp.sum(received[:, rows * flat_width])
    grad_flat = received[:, : rows * flat_width].reshape(-1)

    grad_rms = jnp.sqrt(square_total / COUNT)
    factor = jnp.minimum(1.0, CLIP_RMS / grad_rms)
    weights, firsts, seconds = adamw(
        master_flat.reshape(-1),
        grad_flat,
        first_moment.reshape(-1),
        second_moment.reshape(-1),
        WDECAY,
        factor,
    )
    gains_new, gain_one, gain_two = adamw(
        gain_master, gain_grad, gain_first, gain_second, 0.0, factor
    )

    lowered = weights.astype(jnp.bfloat16).reshape(shard_count, rows * flat_width)
    returned = lax.all_to_all(lowered, "shard", split_axis=0, concat_axis=0, tiled=True)
    returned = returned.reshape(shard_count, rows, flat_width)
    copies = []
    offset = 0
    for group_width in group_widths:
        section = returned[:, :, offset : offset + group_width]
        copies.append(jnp.transpose(section, (1, 0, 2)).reshape(rows, shard_count * group_width))
        offset = offset + group_width
    gain_copy = gains_new.astype(jnp.bfloat16)
    return (
        weights.reshape(master_flat.shape),
        firsts.reshape(master_flat.shape),
        seconds.reshape(master_flat.shape),
        gains_new,
        gain_one,
        gain_two,
        copies[0],
        copies[1],
        copies[2],
        copies[3],
        copies[4],
        copies[5],
        copies[6],
        gain_copy,
        grad_rms,
    )


def solution(mesh):
    return jax.shard_map(
        shards,
        mesh=mesh,
        in_specs=(
            P(None, "shard", "tensor"),
            P(None, "shard", "tensor"),
            P(None, "shard", "tensor"),
            P(None, "shard", "tensor"),
            P(None, "shard", "tensor"),
            P(None, "shard", "tensor"),
            P(None, "shard", "tensor"),
            P(None, "tensor", None, "shard"),
            P("shard", "tensor", None),
            P("shard", "tensor", None),
            P("shard", "tensor", None),
            P(None, "shard"),
            P(None, "shard"),
            P(None, "shard"),
        ),
        out_specs=(
            P("shard", "tensor", None),
            P("shard", "tensor", None),
            P("shard", "tensor", None),
            P(None, "shard"),
            P(None, "shard"),
            P(None, "shard"),
            P("shard", "tensor"),
            P("shard", "tensor"),
            P("shard", "tensor"),
            P("shard", "tensor"),
            P("shard", "tensor"),
            P("shard", "tensor"),
            P("shard", "tensor"),
            P(None, "shard"),
            P(),
        ),
        check_vma=False,
    )
```

profile of v0, /device:TPU:1, one launch (start us, length us, event | category | flops | bytes accessed | tf_op | source)
XLA Modules:
  0.0 102.4 jit_solution(9435263676566376199)
XLA Ops:
  0.7 0.9 convert_reduce_fusion.5
  1.6 0.8 copy-done.7
  2.4 0.6 multiply_reduce_fusion.6
  3.0 0.6 multiply_reduce_fusion.5
  3.7 0.6 multiply_reduce_fusion.4
  4.6 0.6 multiply_reduce_fusion.3
  5.5 0.6 multiply_reduce_fusion.2
  6.3 0.6 multiply_reduce_fusion.7
  11.5 9.3 %psum.7 = f32[33]{0:T(128)S(1)} all-reduce(f32[33]{0:T(128)S(1)} %pad_maximum_fusion), channel_id=1, replica_groups=mesh['shard'=128,'tensor'=4] {'tensor'}, use_global_device_ids=true, to_apply=%region_15.0 | all-reduce | flops 33 | bytes 264 | tf_op jit(solution)/shard_map/psum | solution.py:73
  21.4 0.6 multiply_reduce_fusion.9
  22.9 1.1 %mul.264 = f32[16,128,10]{2,1,0:T(8,128)S(1)} reshape(f32[16,1280]{1,0:T(8,128)S(1)} %get-tuple-element.81) | data formatting | bytes 163840 | tf_op jit(solution)/shard_map/mul | solution.py:32
  24.3 1.1 %mul.266 = f32[16,128,10]{2,1,0:T(8,128)S(1)} reshape(f32[16,1280]{1,0:T(8,128)S(1)} %get-tuple-element.79) | data formatting | bytes 163840 | tf_op jit(solution)/shard_map/mul | solution.py:32
  25.7 1.1 %mul.268 = f32[16,128,10]{2,1,0:T(8,128)S(1)} reshape(f32[16,1280]{1,0:T(8,128)S(1)} %get-tuple-element.77) | data formatting | bytes 163840 | tf_op jit(solution)/shard_map/mul | solution.py:32
  28.7 1.3 %copy.88 = f32[128,1,737]{2,1,0:T(1,128)} copy(f32[128,1,737]{0,2,1:T(8,128)S(1)} %pad_bitcast_fusion) | data formatting | bytes 754688 | tf_op jit(solution)/shard_map/all_to_all | solution.py:81
  30.0 19.7 %all-to-all-start = ((f32[128,1,737]{2,1,0:T(1,128)}), f32[128,1,737]{2,1,0:T(1,128)S(1)}, u32[]{:S(2)}, u32[]{:S(2)}) async-start(f32[128,1,737]{2,1,0:T(1,128)} %copy.88), calls=%async_computation | async-start | bytes 786432 | tf_op jit(solution)/shard_map/all_to_all | solution.py:81
  49.8 2.3 %multiply_reduce_fusion = (f32[94208]{0:T(1024)S(1)}, f32[94208]{0:T(1024)S(1)}) fusion(f32[1,1,94208]{2,1,0:T(1,128)S(1)} %copy-done.1, f32[1,1,94208]{2,1,0:T(1,128)S(1)} %copy-done.2), kind=kLoop, calls=%fused_computation.17 | loop fusion | flops 188416 | bytes 1507328 | tf_op jit(solution)/shard_map/mul | solution.py:22
  53.8 1.5 %reduce.13 = f32[94208]{0:T(1024)S(1)} reduce(f32[1,1,94208]{2,1,0:T(1,128)S(1)} %copy-done, f32[]{:T(128)} %broadcast.117), dimensions={0,1}, to_apply=%param.22.reduce_sub_computation.3 | reduce | bytes 753668 | tf_op args[8]
  55.7 11.9 %all-to-all-done = f32[128,1,737]{2,1,0:T(1,128)S(1)} async-done(((f32[128,1,737]{2,1,0:T(1,128)}), f32[128,1,737]{2,1,0:T(1,128)S(1)}, u32[]{:S(2)}, u32[]{:S(2)}) %all-to-all-start) | async-done | bytes 377376 | tf_op jit(solution)/shard_map/all_to_all | solution.py:81
  67.6 0.7 copy.89
  70.5 0.7 reduce.14
  71.3 0.9 reshape.173
  72.2 5.6 %all-to-all-start.1 = ((bf16[128,2,368]{2,1,0:T(2,128)(2,1)}), bf16[128,2,368]{2,1,0:T(2,128)(2,1)S(1)}, u32[]{:S(2)}, u32[]{:S(2)}) async-start(bf16[128,2,368]{2,1,0:T(2,128)(2,1)} %reshape.173), calls=%async_computation.1 | async-start | bytes 393216 | tf_op jit(solution)/shard_map/all_to_all | solution.py:100
  78.7 3.5 %multiply_subtract_fusion = (f32[1,1,94208]{2,1,0:T(1,128)}, f32[1,1,94208]{2,1,0:T(1,128)}, f32[1,1,94208]{2,1,0:T(1,128)}) fusion(f32[1,1,94208]{2,1,0:T(1,128)S(1)} %copy-done, f32[1,1,94208]{2,1,0:T(1,128)S(1)} %mul.281, f32[1,1,94208]{2,1,0:T(1,128)S(1)} %copy-done.2, f32[1,1,94208]{2,1,0:T(1,128)S(1)} %copy-done.1), kind=kLoop, calls=%fused_computation.12 | loop fusion | flops 1413120 | bytes 2637824 | tf_op jit(solution)/shard_map/sub | solution.py:28
  83.4 8.5 %all-to-all-done.1 = bf16[128,2,368]{2,1,0:T(2,128)(2,1)S(1)} async-done(((bf16[128,2,368]{2,1,0:T(2,128)(2,1)}), bf16[128,2,368]{2,1,0:T(2,128)(2,1)S(1)}, u32[]{:S(2)}, u32[]{:S(2)}) %all-to-all-start.1) | async-done | bytes 188448 | tf_op jit(solution)/shard_map/all_to_all | solution.py:100
  92.3 0.7 copy.96
  93.3 0.7 copy.104
  94.1 0.7 copy.105
  94.9 0.7 copy.106
  95.8 0.7 copy.107
  96.8 1.3 %reshape.151 = bf16[16,1280]{1,0:T(8,128)(2,1)} reshape(bf16[16,128,10]{2,1,0:T(8,128)(2,1)S(1)} %copy.101) | data formatting | bytes 81920 | tf_op jit(solution)/shard_map/reshape | solution.py:106
  98.4 1.3 %reshape.152 = bf16[16,1280]{1,0:T(8,128)(2,1)} reshape(bf16[16,128,10]{2,1,0:T(8,128)(2,1)S(1)} %copy.102) | data formatting | bytes 81920 | tf_op jit(solution)/shard_map/reshape | solution.py:106
  100.0 1.3 %reshape.153 = bf16[16,1280]{1,0:T(8,128)(2,1)} reshape(bf16[16,128,10]{2,1,0:T(8,128)(2,1)S(1)} %copy.103) | data formatting | bytes 81920 | tf_op jit(solution)/shard_map/reshape | solution.py:106
  (83 shorter events, 11.2 us)
Async XLA Ops:
  0.6 0.9 copy-start.6
  1.6 0.8 copy-start.7
  1.6 1.5 %copy-start.8 = (bf16[4,16,512]{2,1,0:T(8,128)(2,1)S(1)}, bf16[4,16,512]{2,1,0:T(8,128)(2,1)}, u32[]{:S(2)}) copy-start(bf16[4,16,512]{2,1,0:T(8,128)(2,1)} %param.17) | copy-start | bytes 196612
  2.4 1.3 %copy-start.3 = (bf16[4,16,1280]{2,1,0:T(8,128)(2,1)S(1)}, bf16[4,16,1280]{2,1,0:T(8,128)(2,1)}, u32[]{:S(2)}) copy-start(bf16[4,16,1280]{2,1,0:T(8,128)(2,1)} %param.18) | copy-start | bytes 491524
  3.7 0.9 copy-start.4
  4.6 0.9 copy-start.5
  5.5 0.7 copy-start.9
  30.0 19.8 %copy-start.1 = (f32[1,1,94208]{2,1,0:T(1,128)S(1)}, f32[1,1,94208]{2,1,0:T(1,128)}, u32[]{:S(2)}) copy-start(f32[1,1,94208]{2,1,0:T(1,128)} %param.24) | copy-start | bytes 1130500
  30.0 19.8 %copy-start.2 = (f32[1,1,94208]{2,1,0:T(1,128)S(1)}, f32[1,1,94208]{2,1,0:T(1,128)}, u32[]{:S(2)}) copy-start(f32[1,1,94208]{2,1,0:T(1,128)} %param.23) | copy-start | bytes 1130500
  30.0 37.6 %all-to-all-start = ((f32[128,1,737]{2,1,0:T(1,128)}), f32[128,1,737]{2,1,0:T(1,128)S(1)}, u32[]{:S(2)}, u32[]{:S(2)}) async-start(f32[128,1,737]{2,1,0:T(1,128)} %copy.88), calls=%async_computation | async-start | bytes 786432 | tf_op jit(solution)/shard_map/all_to_all | solution.py:81
  52.8 1.0 copy-start
  72.2 19.7 %all-to-all-start.1 = ((bf16[128,2,368]{2,1,0:T(2,128)(2,1)}), bf16[128,2,368]{2,1,0:T(2,128)(2,1)S(1)}, u32[]{:S(2)}, u32[]{:S(2)}) async-start(bf16[128,2,368]{2,1,0:T(2,128)(2,1)} %reshape.173), calls=%async_computation.1 | async-start | bytes 393216 | tf_op jit(solution)/shard_map/all_to_all | solution.py:100
  78.7 3.6 %copy-start.11 = (f32[2,16]{1,0:T(2,128)S(1)}, f32[2,16]{1,0:T(2,128)}, u32[]{:S(2)}) copy-start(f32[2,16]{1,0:T(2,128)} %param.26) | copy-start | bytes 388
  78.7 3.6 %copy-start.12 = (f32[2,16]{1,0:T(2,128)S(1)}, f32[2,16]{1,0:T(2,128)}, u32[]{:S(2)}) copy-start(f32[2,16]{1,0:T(2,128)} %param.27) | copy-start | bytes 388
  82.2 0.7 copy-start.10
where the time goes:
time: 103 us; the launch traced here: 102 us
  starting transfers between devices  25.4 us (25%)
  local copies, waits for them, and re-layouts  23.7 us (23%)
  waiting for transfers between devices  20.4 us (20%)
  other arithmetic  14.9 us (14%)
  blocking collectives  9.26 us (9%)
  between operations  8.75 us (8%)
    all_to_all x1, starting transfers between devices, shards(): lax.all_to_all(payload, 'shard', split_axis=0, concat_axis=0, tiled=True)  19.7 us
    all_to_all x1, waiting for transfers between devices, shards(): lax.all_to_all(payload, 'shard', split_axis=0, concat_axis=0, tiled=True)  11.9 us
    psum x1, blocking collectives, shards(): lax.psum(jnp.concatenate([gain_local.reshape(-1), block_square.reshape(1)...  9.26 us
    all_to_all x1, waiting for transfers between devices, shards(): lax.all_to_all(lowered, 'shard', split_axis=0, concat_axis=0, tiled=True)  8.51 us
    unnamed x40, local copies, waits for them, and re-layouts  7.03 us
    all_to_all x1, starting transfers between devices, shards(): lax.all_to_all(lowered, 'shard', split_axis=0, concat_axis=0, tiled=True)  5.64 us
    mul x14, local copies, waits for them, and re-layouts, mean_block(): return jnp.sum(matrix.astype(jnp.float32), axis=0) * (1.0 / MB)  5.12 us
    reshape x3, local copies, waits for them, and re-layouts, shards(): jnp.transpose(section, (1, 0, 2)).reshape(rows, shard_count * group_width)  3.86 us
  transfers between devices with their start and end apart: 2, of which 2 were waited for; matrix products, arithmetic and copies ran while one was open for 10% of the time, Pallas kernels for 0%

commit v1 on v0

--- a/solution.py
+++ b/solution.py
@@ -41,6 +41,18 @@
     return jnp.transpose(joined, (1, 0, 2)).reshape(shard_count, -1)
 
 
+def tensor_sum(value):
+    count = lax.axis_size("tensor")
+    if count & (count - 1):
+        return lax.psum(value, "tensor")
+    step = 1
+    while step < count:
+        pairs = [(index, index ^ step) for index in range(count)]
+        value = value + lax.ppermute(value, "tensor", pairs)
+        step = step * 2
+    return value
+
+
 def shards(
     grad_query,
     grad_key,
@@ -64,15 +76,18 @@
     flat_width = sum(group_widths)
 
     group_means = [mean_block(matrix) for matrix in blocks]
-    block_square = jnp.sum(group_means[0] * group_means[0])
+    lanes = 128
+    block_square = jnp.sum((group_means[0] * group_means[0]).reshape(-1, lanes), axis=0)
     for averaged in group_means[1:]:
-        block_square = block_square + jnp.sum(averaged * averaged)
+        block_square = block_square + jnp.sum((averaged * averaged).reshape(-1, lanes), axis=0)
 
     gain_local = jnp.sum(grad_norms.astype(jnp.float32), axis=(0, 1))
     gain_size = gain_local.size
-    summed = lax.psum(jnp.concatenate([gain_local.reshape(-1), block_square.reshape(1)]), "tensor")
+    summed = tensor_sum(jnp.concatenate([gain_local.reshape(-1), block_square]))
     gain_grad = summed[:gain_size].reshape(gain_local.shape) * (1.0 / MB)
-    shard_square = summed[gain_size] + jnp.sum(gain_grad * gain_grad)
+    shard_square = jnp.sum(
+        jnp.concatenate([summed[gain_size:], (gain_grad * gain_grad).reshape(-1)])
+    )
 
     payload = by_destination(group_means, shard_count)
     payload = jnp.concatenate(

time: 103 us -> 99.3 us (0.964)
  blocking collectives: 9.26 us -> 0 us
  starting transfers between devices: 25.4 us -> 33.1 us
  between operations: 8.75 us -> 4.37 us
  local copies, waits for them, and re-layouts: 23.7 us -> 27.2 us
  other arithmetic: 14.9 us -> 12.3 us
  waiting for transfers between devices: 20.4 us -> 21.7 us
    psum x1 -> x0, blocking collectives: 9.26 us -> none  [shards(): lax.psum(jnp.concatenate([gain_local.reshape(-1), block_square.reshape(1)...]
    ppermute x0 -> x2, starting transfers between devices: none -> 8.28 us  [tensor_sum(): value = value + lax.ppermute(value, 'tensor', pairs)]
    unnamed x40, local copies, waits for them, and re-layouts: 7.03 us -> 11.1 us
    reduce_sum x7 -> x9, other arithmetic: 4.29 us -> 1.48 us  [the longest x2 1.27 us: shards(): jnp.sum(jnp.concatenate([summed[gain_size:], (gain_grad * gain_grad).resh...]
    ppermute x0 -> x2, waiting for transfers between devices: none -> 1.28 us  [tensor_sum(): value = value + lax.ppermute(value, 'tensor', pairs)]
  transfers between devices with their start and end apart: 2 -> 4, of which waited for: 2 -> 3; matrix products, arithmetic and copies ran while one was open for 10% -> 16% of each run, Pallas kernels for 0% -> 0%
where the time goes in v1:
time: 99.3 us; the launch traced here: 98.7 us
  starting transfers between devices  33.1 us (33%)
  local copies, waits for them, and re-layouts  27.2 us (27%)
  waiting for transfers between devices  21.7 us (22%)
  other arithmetic  12.3 us (12%)
  between operations  4.37 us (4%)
    all_to_all x1, starting transfers between devices, shards(): lax.all_to_all(payload, 'shard', split_axis=0, concat_axis=0, tiled=True)  19.2 us
    all_to_all x1, waiting for transfers between devices, shards(): lax.all_to_all(payload, 'shard', split_axis=0, concat_axis=0, tiled=True)  11.9 us
    unnamed x40, local copies, waits for them, and re-layouts  11.1 us
    all_to_all x1, waiting for transfers between devices, shards(): lax.all_to_all(lowered, 'shard', split_axis=0, concat_axis=0, tiled=True)  8.51 us
    ppermute x2, starting transfers between devices, tensor_sum(): value = value + lax.ppermute(value, 'tensor', pairs)  8.28 us
    all_to_all x1, starting transfers between devices, shards(): lax.all_to_all(lowered, 'shard', split_axis=0, concat_axis=0, tiled=True)  5.64 us
    mul x14, local copies, waits for them, and re-layouts, mean_block(): return jnp.sum(matrix.astype(jnp.float32), axis=0) * (1.0 / MB)  5.1 us
    reshape x3, local copies, waits for them, and re-layouts, shards(): jnp.transpose(section, (1, 0, 2)).reshape(rows, shard_count * group_width)  3.86 us
  transfers between devices with their start and end apart: 4, of which 3 were waited for; matrix products, arithmetic and copies ran while one was open for 16% of the time, Pallas kernels for 0%

profile of v1, /device:TPU:1, one launch (start us, length us, event | category | flops | bytes accessed | tf_op | source)
XLA Modules:
  0.0 98.7 jit_solution(7044684637590464420)
XLA Ops:
  0.6 0.9 convert_reduce_fusion.2
  1.6 0.9 copy-done.3
  2.7 0.8 copy-done.4
  3.6 0.8 copy-done.5
  4.5 0.8 copy-done.6
  5.3 0.8 copy-done.7
  6.2 0.8 copy-done.8
  7.9 3.9 %collective-permute-start = (f32[160]{0:T(256)S(1)}, f32[160]{0:T(256)S(1)}, u32[]{:S(2)}, u32[]{:S(2)}) collective-permute-start(f32[160]{0:T(256)S(1)} %pad_maximum_fusion), channel_id=1, source_target_pairs={{0,1},{1,0},{2,3},{3,2},{4,5},{5,4},{6,7},{7,6},{8,9},{9,8},{10,11... | collective-permute-start | bytes 1928 | tf_op jit(solution)/shard_map/ppermute | solution.py:51
  12.8 1.1 %mul.306 = f32[16,128,10]{2,1,0:T(8,128)S(1)} reshape(f32[16,1280]{1,0:T(8,128)S(1)} %get-tuple-element.92) | data formatting | bytes 163840 | tf_op jit(solution)/shard_map/mul | solution.py:32
  14.2 1.1 %mul.308 = f32[16,128,10]{2,1,0:T(8,128)S(1)} reshape(f32[16,1280]{1,0:T(8,128)S(1)} %get-tuple-element.94) | data formatting | bytes 163840 | tf_op jit(solution)/shard_map/mul | solution.py:32
  15.7 1.1 %mul.310 = f32[16,128,10]{2,1,0:T(8,128)S(1)} reshape(f32[16,1280]{1,0:T(8,128)S(1)} %get-tuple-element.96) | data formatting | bytes 163840 | tf_op jit(solution)/shard_map/mul | solution.py:32
  17.2 4.4 %collective-permute-start.1 = (f32[160]{0:T(256)S(1)}, f32[160]{0:T(256)S(1)}, u32[]{:S(2)}, u32[]{:S(2)}) collective-permute-start(f32[160]{0:T(256)S(1)} %fusion.9), channel_id=1, source_target_pairs={{0,2},{1,3},{2,0},{3,1},{4,6},{5,7},{6,4},{7,5},{8,10},{9,11},{10,... | collective-permute-start | bytes 1928 | tf_op jit(solution)/shard_map/ppermute | solution.py:51
  21.7 1.3 %collective-permute-done.1 = f32[160]{0:T(256)S(1)} collective-permute-done((f32[160]{0:T(256)S(1)}, f32[160]{0:T(256)S(1)}, u32[]{:S(2)}, u32[]{:S(2)}) %collective-permute-start.1) | collective-permute-done | bytes 672 | tf_op jit(solution)/shard_map/ppermute | solution.py:51
  23.6 0.7 slice_reduce_fusion.1
  25.6 1.3 %copy.113 = f32[128,1,737]{2,1,0:T(1,128)} copy(f32[128,1,737]{0,2,1:T(8,128)S(1)} %pad_bitcast_fusion) | data formatting | bytes 754688 | tf_op jit(solution)/shard_map/all_to_all | solution.py:96
  26.9 19.2 %all-to-all-start = ((f32[128,1,737]{2,1,0:T(1,128)}), f32[128,1,737]{2,1,0:T(1,128)S(1)}, u32[]{:S(2)}, u32[]{:S(2)}) async-start(f32[128,1,737]{2,1,0:T(1,128)} %copy.113), calls=%async_computation | async-start | bytes 786432 | tf_op jit(solution)/shard_map/all_to_all | solution.py:96
  46.1 2.3 %multiply_reduce_fusion = (f32[94208]{0:T(1024)S(1)}, f32[94208]{0:T(1024)S(1)}) fusion(f32[1,1,94208]{2,1,0:T(1,128)S(1)} %copy-done.1, f32[1,1,94208]{2,1,0:T(1,128)S(1)} %copy-done.2), kind=kLoop, calls=%fused_computation.17 | loop fusion | flops 188416 | bytes 1507328 | tf_op jit(solution)/shard_map/mul | solution.py:22
  50.1 1.5 %reduce.16 = f32[94208]{0:T(1024)S(1)} reduce(f32[1,1,94208]{2,1,0:T(1,128)S(1)} %copy-done, f32[]{:T(128)} %broadcast.134), dimensions={0,1}, to_apply=%param.22.reduce_sub_computation.3 | reduce | bytes 753668 | tf_op args[8]
  52.0 11.9 %all-to-all-done = f32[128,1,737]{2,1,0:T(1,128)S(1)} async-done(((f32[128,1,737]{2,1,0:T(1,128)}), f32[128,1,737]{2,1,0:T(1,128)S(1)}, u32[]{:S(2)}, u32[]{:S(2)}) %all-to-all-start) | async-done | bytes 377376 | tf_op jit(solution)/shard_map/all_to_all | solution.py:96
  63.9 0.7 copy.114
  66.7 0.7 reduce.17
  67.6 0.9 reshape.216
  68.5 5.6 %all-to-all-start.1 = ((bf16[128,2,368]{2,1,0:T(2,128)(2,1)}), bf16[128,2,368]{2,1,0:T(2,128)(2,1)S(1)}, u32[]{:S(2)}, u32[]{:S(2)}) async-start(bf16[128,2,368]{2,1,0:T(2,128)(2,1)} %reshape.216), calls=%async_computation.1 | async-start | bytes 393216 | tf_op jit(solution)/shard_map/all_to_all | solution.py:115
  75.0 3.5 %multiply_subtract_fusion = (f32[1,1,94208]{2,1,0:T(1,128)}, f32[1,1,94208]{2,1,0:T(1,128)}, f32[1,1,94208]{2,1,0:T(1,128)}) fusion(f32[1,1,94208]{2,1,0:T(1,128)S(1)} %copy-done, f32[1,1,94208]{2,1,0:T(1,128)S(1)} %mul.330, f32[1,1,94208]{2,1,0:T(1,128)S(1)} %copy-done.2, f32[1,1,94208]{2,1,0:T(1,128)S(1)} %copy-done.1), kind=kLoop, calls=%fused_computation.12 | loop fusion | flops 1413120 | bytes 2637824 | tf_op jit(solution)/shard_map/sub | solution.py:28
  79.7 8.5 %all-to-all-done.1 = bf16[128,2,368]{2,1,0:T(2,128)(2,1)S(1)} async-done(((bf16[128,2,368]{2,1,0:T(2,128)(2,1)}), bf16[128,2,368]{2,1,0:T(2,128)(2,1)S(1)}, u32[]{:S(2)}, u32[]{:S(2)}) %all-to-all-start.1) | async-done | bytes 188448 | tf_op jit(solution)/shard_map/all_to_all | solution.py:115
  89.7 1.3 %reshape.194 = bf16[16,1280]{1,0:T(8,128)(2,1)} reshape(bf16[16,128,10]{2,1,0:T(8,128)(2,1)S(1)} %copy.126) | data formatting | bytes 81920 | tf_op jit(solution)/shard_map/reshape | solution.py:121
  91.3 1.3 %reshape.195 = bf16[16,1280]{1,0:T(8,128)(2,1)} reshape(bf16[16,128,10]{2,1,0:T(8,128)(2,1)S(1)} %copy.127) | data formatting | bytes 81920 | tf_op jit(solution)/shard_map/reshape | solution.py:121
  92.9 1.3 %reshape.196 = bf16[16,1280]{1,0:T(8,128)(2,1)} reshape(bf16[16,128,10]{2,1,0:T(8,128)(2,1)S(1)} %copy.128) | data formatting | bytes 81920 | tf_op jit(solution)/shard_map/reshape | solution.py:121
  94.3 0.7 copy.129
  95.2 0.7 copy.130
  96.0 0.7 copy.131
  96.8 0.7 copy.132
  (104 shorter events, 12.4 us)
Async XLA Ops:
  1.6 0.9 copy-start.3
  2.6 0.9 copy-start.4
  3.5 0.8 copy-start.5
  4.4 0.8 copy-start.6
  5.3 0.8 copy-start.7
  6.2 0.8 copy-start.8
  7.0 0.7 copy-start.9
  7.9 9.2 %collective-permute-start = (f32[160]{0:T(256)S(1)}, f32[160]{0:T(256)S(1)}, u32[]{:S(2)}, u32[]{:S(2)}) collective-permute-start(f32[160]{0:T(256)S(1)} %pad_maximum_fusion), channel_id=1, source_target_pairs={{0,1},{1,0},{2,3},{3,2},{4,5},{5,4},{6,7},{7,6},{8,9},{9,8},{10,11... | collective-permute-start | bytes 1928 | tf_op jit(solution)/shard_map/ppermute | solution.py:51
  17.2 5.8 %collective-permute-start.1 = (f32[160]{0:T(256)S(1)}, f32[160]{0:T(256)S(1)}, u32[]{:S(2)}, u32[]{:S(2)}) collective-permute-start(f32[160]{0:T(256)S(1)} %fusion.9), channel_id=1, source_target_pairs={{0,2},{1,3},{2,0},{3,1},{4,6},{5,7},{6,4},{7,5},{8,10},{9,11},{10,... | collective-permute-start | bytes 1928 | tf_op jit(solution)/shard_map/ppermute | solution.py:51
  26.9 19.2 %copy-start.1 = (f32[1,1,94208]{2,1,0:T(1,128)S(1)}, f32[1,1,94208]{2,1,0:T(1,128)}, u32[]{:S(2)}) copy-start(f32[1,1,94208]{2,1,0:T(1,128)} %param.24) | copy-start | bytes 1130500
  26.9 19.2 %copy-start.2 = (f32[1,1,94208]{2,1,0:T(1,128)S(1)}, f32[1,1,94208]{2,1,0:T(1,128)}, u32[]{:S(2)}) copy-start(f32[1,1,94208]{2,1,0:T(1,128)} %param.23) | copy-start | bytes 1130500
  26.9 37.0 %all-to-all-start = ((f32[128,1,737]{2,1,0:T(1,128)}), f32[128,1,737]{2,1,0:T(1,128)S(1)}, u32[]{:S(2)}, u32[]{:S(2)}) async-start(f32[128,1,737]{2,1,0:T(1,128)} %copy.113), calls=%async_computation | async-start | bytes 786432 | tf_op jit(solution)/shard_map/all_to_all | solution.py:96
  49.1 1.0 %copy-start = (f32[1,1,94208]{2,1,0:T(1,128)S(1)}, f32[1,1,94208]{2,1,0:T(1,128)}, u32[]{:S(2)}) copy-start(f32[1,1,94208]{2,1,0:T(1,128)} %param.22) | copy-start | bytes 1130500
  68.5 19.7 %all-to-all-start.1 = ((bf16[128,2,368]{2,1,0:T(2,128)(2,1)}), bf16[128,2,368]{2,1,0:T(2,128)(2,1)S(1)}, u32[]{:S(2)}, u32[]{:S(2)}) async-start(bf16[128,2,368]{2,1,0:T(2,128)(2,1)} %reshape.216), calls=%async_computation.1 | async-start | bytes 393216 | tf_op jit(solution)/shard_map/all_to_all | solution.py:115
  74.9 3.6 %copy-start.11 = (f32[2,16]{1,0:T(2,128)S(1)}, f32[2,16]{1,0:T(2,128)}, u32[]{:S(2)}) copy-start(f32[2,16]{1,0:T(2,128)} %param.26) | copy-start | bytes 388
  75.0 3.6 %copy-start.12 = (f32[2,16]{1,0:T(2,128)S(1)}, f32[2,16]{1,0:T(2,128)}, u32[]{:S(2)}) copy-start(f32[2,16]{1,0:T(2,128)} %param.27) | copy-start | bytes 388
  78.5 0.7 copy-start.10

commit v2 on v1

--- a/solution.py
+++ b/solution.py
@@ -43,13 +43,15 @@
 
 def tensor_sum(value):
     count = lax.axis_size("tensor")
-    if count & (count - 1):
+    if count == 4:
+        masks = (1, 3)
+    elif count & (count - 1) == 0:
+        masks = tuple(1 << bit for bit in range(count.bit_length() - 1))
+    else:
         return lax.psum(value, "tensor")
-    step = 1
-    while step < count:
-        pairs = [(index, index ^ step) for index in range(count)]
+    for mask in masks:
+        pairs = [(index, index ^ mask) for index in range(count)]
         value = value + lax.ppermute(value, "tensor", pairs)
-        step = step * 2
     return value
 
 
@@ -85,8 +87,9 @@
     gain_size = gain_local.size
     summed = tensor_sum(jnp.concatenate([gain_local.reshape(-1), block_square]))
     gain_grad = summed[:gain_size].reshape(gain_local.shape) * (1.0 / MB)
+    gain_square = (gain_grad * gain_grad).reshape(-1)
     shard_square = jnp.sum(
-        jnp.concatenate([summed[gain_size:], (gain_grad * gain_grad).reshape(-1)])
+        summed[gain_size:] + jnp.pad(gain_square, (0, lanes - gain_size))
     )
 
     payload = by_destination(group_means, shard_count)

time: 99.3 us -> 97.8 us (0.985)
  between operations: 4.37 us -> 3.07 us
where the time goes in v2:
time: 97.8 us; the launch traced here: 97.1 us
  starting transfers between devices  32.4 us (33%)
  local copies, waits for them, and re-layouts  27.9 us (29%)
  waiting for transfers between devices  22 us (22%)
  other arithmetic  11.7 us (12%)
  between operations  3.07 us (3%)
    all_to_all x1, starting transfers between devices, shards(): lax.all_to_all(payload, 'shard', split_axis=0, concat_axis=0, tiled=True)  19.2 us
    all_to_all x1, waiting for transfers between devices, shards(): lax.all_to_all(payload, 'shard', split_axis=0, concat_axis=0, tiled=True)  11.9 us
    unnamed x40, local copies, waits for them, and re-layouts  11.1 us
    all_to_all x1, waiting for transfers between devices, shards(): lax.all_to_all(lowered, 'shard', split_axis=0, concat_axis=0, tiled=True)  8.51 us
    ppermute x2, starting transfers between devices, tensor_sum(): value = value + lax.ppermute(value, 'tensor', pairs)  7.64 us
    all_to_all x1, starting transfers between devices, shards(): lax.all_to_all(lowered, 'shard', split_axis=0, concat_axis=0, tiled=True)  5.64 us
    mul x14, local copies, waits for them, and re-layouts, mean_block(): return jnp.sum(matrix.astype(jnp.float32), axis=0) * (1.0 / MB)  5.1 us
    reshape x3, local copies, waits for them, and re-layouts, shards(): jnp.transpose(section, (1, 0, 2)).reshape(rows, shard_count * group_width)  3.86 us
  transfers between devices with their start and end apart: 4, of which 3 were waited for; matrix products, arithmetic and copies ran while one was open for 16% of the time, Pallas kernels for 0%

profile of v2, /device:TPU:1, one launch (start us, length us, event | category | flops | bytes accessed | tf_op | source)
XLA Modules:
  0.0 97.1 jit_solution(5796424165561836432)
XLA Ops:
  0.6 0.9 convert_reduce_fusion.2
  1.6 0.9 copy-done.3
  2.7 0.8 copy-done.4
  3.6 0.8 copy-done.5
  4.5 0.8 copy-done.6
  5.3 0.8 copy-done.7
  6.2 0.8 copy-done.8
  7.9 3.9 %collective-permute-start = (f32[160]{0:T(256)S(1)}, f32[160]{0:T(256)S(1)}, u32[]{:S(2)}, u32[]{:S(2)}) collective-permute-start(f32[160]{0:T(256)S(1)} %pad_maximum_fusion), channel_id=1, source_target_pairs={{0,1},{1,0},{2,3},{3,2},{4,5},{5,4},{6,7},{7,6},{8,9},{9,8},{10,11... | collective-permute-start | bytes 1928 | tf_op jit(solution)/shard_map/ppermute | solution.py:54
  12.8 1.1 %mul.306 = f32[16,128,10]{2,1,0:T(8,128)S(1)} reshape(f32[16,1280]{1,0:T(8,128)S(1)} %get-tuple-element.92) | data formatting | bytes 163840 | tf_op jit(solution)/shard_map/mul | solution.py:32
  14.2 1.1 %mul.308 = f32[16,128,10]{2,1,0:T(8,128)S(1)} reshape(f32[16,1280]{1,0:T(8,128)S(1)} %get-tuple-element.94) | data formatting | bytes 163840 | tf_op jit(solution)/shard_map/mul | solution.py:32
  15.7 1.1 %mul.310 = f32[16,128,10]{2,1,0:T(8,128)S(1)} reshape(f32[16,1280]{1,0:T(8,128)S(1)} %get-tuple-element.96) | data formatting | bytes 163840 | tf_op jit(solution)/shard_map/mul | solution.py:32
  17.2 3.7 %collective-permute-start.1 = (f32[160]{0:T(256)S(1)}, f32[160]{0:T(256)S(1)}, u32[]{:S(2)}, u32[]{:S(2)}) collective-permute-start(f32[160]{0:T(256)S(1)} %fusion.9), channel_id=1, source_target_pairs={{0,3},{1,2},{2,1},{3,0},{4,7},{5,6},{6,5},{7,4},{8,11},{9,10},{10,... | collective-permute-start | bytes 1928 | tf_op jit(solution)/shard_map/ppermute | solution.py:54
  21.1 1.6 %collective-permute-done.1 = f32[160]{0:T(256)S(1)} collective-permute-done((f32[160]{0:T(256)S(1)}, f32[160]{0:T(256)S(1)}, u32[]{:S(2)}, u32[]{:S(2)}) %collective-permute-start.1) | collective-permute-done | bytes 672 | tf_op jit(solution)/shard_map/ppermute | solution.py:54
  22.7 0.7 add_reduce_fusion
  23.4 0.7 pad_bitcast_fusion
  24.1 1.3 %copy.113 = f32[128,1,737]{2,1,0:T(1,128)} copy(f32[128,1,737]{0,2,1:T(8,128)S(1)} %pad_bitcast_fusion) | data formatting | bytes 754688 | tf_op jit(solution)/shard_map/all_to_all | solution.py:99
  25.4 19.2 %all-to-all-start = ((f32[128,1,737]{2,1,0:T(1,128)}), f32[128,1,737]{2,1,0:T(1,128)S(1)}, u32[]{:S(2)}, u32[]{:S(2)}) async-start(f32[128,1,737]{2,1,0:T(1,128)} %copy.113), calls=%async_computation | async-start | bytes 786432 | tf_op jit(solution)/shard_map/all_to_all | solution.py:99
  44.5 2.3 %multiply_reduce_fusion = (f32[94208]{0:T(1024)S(1)}, f32[94208]{0:T(1024)S(1)}) fusion(f32[1,1,94208]{2,1,0:T(1,128)S(1)} %copy-done.1, f32[1,1,94208]{2,1,0:T(1,128)S(1)} %copy-done.2), kind=kLoop, calls=%fused_computation.17 | loop fusion | flops 188416 | bytes 1507328 | tf_op jit(solution)/shard_map/mul | solution.py:22
  48.5 1.5 %reduce.12 = f32[94208]{0:T(1024)S(1)} reduce(f32[1,1,94208]{2,1,0:T(1,128)S(1)} %copy-done, f32[]{:T(128)} %broadcast.136), dimensions={0,1}, to_apply=%param.22.reduce_sub_computation.3 | reduce | bytes 753668 | tf_op args[8]
  50.5 11.9 %all-to-all-done = f32[128,1,737]{2,1,0:T(1,128)S(1)} async-done(((f32[128,1,737]{2,1,0:T(1,128)}), f32[128,1,737]{2,1,0:T(1,128)S(1)}, u32[]{:S(2)}, u32[]{:S(2)}) %all-to-all-start) | async-done | bytes 377376 | tf_op jit(solution)/shard_map/all_to_all | solution.py:99
  65.2 0.7 reduce.13
  66.1 0.9 reshape.217
  67.0 5.6 %all-to-all-start.1 = ((bf16[128,2,368]{2,1,0:T(2,128)(2,1)}), bf16[128,2,368]{2,1,0:T(2,128)(2,1)S(1)}, u32[]{:S(2)}, u32[]{:S(2)}) async-start(bf16[128,2,368]{2,1,0:T(2,128)(2,1)} %reshape.217), calls=%async_computation.1 | async-start | bytes 393216 | tf_op jit(solution)/shard_map/all_to_all | solution.py:118
  73.4 3.5 %multiply_subtract_fusion = (f32[1,1,94208]{2,1,0:T(1,128)}, f32[1,1,94208]{2,1,0:T(1,128)}, f32[1,1,94208]{2,1,0:T(1,128)}) fusion(f32[1,1,94208]{2,1,0:T(1,128)S(1)} %copy-done, f32[1,1,94208]{2,1,0:T(1,128)S(1)} %mul.330, f32[1,1,94208]{2,1,0:T(1,128)S(1)} %copy-done.2, f32[1,1,94208]{2,1,0:T(1,128)S(1)} %copy-done.1), kind=kLoop, calls=%fused_computation.12 | loop fusion | flops 1413120 | bytes 2637824 | tf_op jit(solution)/shard_map/sub | solution.py:28
  78.2 8.5 %all-to-all-done.1 = bf16[128,2,368]{2,1,0:T(2,128)(2,1)S(1)} async-done(((bf16[128,2,368]{2,1,0:T(2,128)(2,1)}), bf16[128,2,368]{2,1,0:T(2,128)(2,1)S(1)}, u32[]{:S(2)}, u32[]{:S(2)}) %all-to-all-start.1) | async-done | bytes 188448 | tf_op jit(solution)/shard_map/all_to_all | solution.py:118
  88.2 1.3 %reshape.195 = bf16[16,1280]{1,0:T(8,128)(2,1)} reshape(bf16[16,128,10]{2,1,0:T(8,128)(2,1)S(1)} %copy.126) | data formatting | bytes 81920 | tf_op jit(solution)/shard_map/reshape | solution.py:124
  89.8 1.3 %reshape.196 = bf16[16,1280]{1,0:T(8,128)(2,1)} reshape(bf16[16,128,10]{2,1,0:T(8,128)(2,1)S(1)} %copy.127) | data formatting | bytes 81920 | tf_op jit(solution)/shard_map/reshape | solution.py:124
  91.4 1.3 %reshape.197 = bf16[16,1280]{1,0:T(8,128)(2,1)} reshape(bf16[16,128,10]{2,1,0:T(8,128)(2,1)S(1)} %copy.128) | data formatting | bytes 81920 | tf_op jit(solution)/shard_map/reshape | solution.py:124
  92.8 0.7 copy.129
  93.6 0.7 copy.130
  94.5 0.7 copy.131
  95.3 0.7 copy.132
  (104 shorter events, 12.4 us)
Async XLA Ops:
  1.6 0.9 copy-start.3
  2.6 0.9 copy-start.4
  3.5 0.8 copy-start.5
  4.4 0.8 copy-start.6
  5.3 0.8 copy-start.7
  6.2 0.8 copy-start.8
  7.0 0.7 copy-start.9
  7.9 9.2 %collective-permute-start = (f32[160]{0:T(256)S(1)}, f32[160]{0:T(256)S(1)}, u32[]{:S(2)}, u32[]{:S(2)}) collective-permute-start(f32[160]{0:T(256)S(1)} %pad_maximum_fusion), channel_id=1, source_target_pairs={{0,1},{1,0},{2,3},{3,2},{4,5},{5,4},{6,7},{7,6},{8,9},{9,8},{10,11... | collective-permute-start | bytes 1928 | tf_op jit(solution)/shard_map/ppermute | solution.py:54
  17.2 5.5 %collective-permute-start.1 = (f32[160]{0:T(256)S(1)}, f32[160]{0:T(256)S(1)}, u32[]{:S(2)}, u32[]{:S(2)}) collective-permute-start(f32[160]{0:T(256)S(1)} %fusion.9), channel_id=1, source_target_pairs={{0,3},{1,2},{2,1},{3,0},{4,7},{5,6},{6,5},{7,4},{8,11},{9,10},{10,... | collective-permute-start | bytes 1928 | tf_op jit(solution)/shard_map/ppermute | solution.py:54
  25.4 19.2 %copy-start.1 = (f32[1,1,94208]{2,1,0:T(1,128)S(1)}, f32[1,1,94208]{2,1,0:T(1,128)}, u32[]{:S(2)}) copy-start(f32[1,1,94208]{2,1,0:T(1,128)} %param.24) | copy-start | bytes 1130500
  25.4 19.2 %copy-start.2 = (f32[1,1,94208]{2,1,0:T(1,128)S(1)}, f32[1,1,94208]{2,1,0:T(1,128)}, u32[]{:S(2)}) copy-start(f32[1,1,94208]{2,1,0:T(1,128)} %param.23) | copy-start | bytes 1130500
  25.4 37.0 %all-to-all-start = ((f32[128,1,737]{2,1,0:T(1,128)}), f32[128,1,737]{2,1,0:T(1,128)S(1)}, u32[]{:S(2)}, u32[]{:S(2)}) async-start(f32[128,1,737]{2,1,0:T(1,128)} %copy.113), calls=%async_computation | async-start | bytes 786432 | tf_op jit(solution)/shard_map/all_to_all | solution.py:99
  47.5 1.0 %copy-start = (f32[1,1,94208]{2,1,0:T(1,128)S(1)}, f32[1,1,94208]{2,1,0:T(1,128)}, u32[]{:S(2)}) copy-start(f32[1,1,94208]{2,1,0:T(1,128)} %param.22) | copy-start | bytes 1130500
  67.0 19.7 %all-to-all-start.1 = ((bf16[128,2,368]{2,1,0:T(2,128)(2,1)}), bf16[128,2,368]{2,1,0:T(2,128)(2,1)S(1)}, u32[]{:S(2)}, u32[]{:S(2)}) async-start(bf16[128,2,368]{2,1,0:T(2,128)(2,1)} %reshape.217), calls=%async_computation.1 | async-start | bytes 393216 | tf_op jit(solution)/shard_map/all_to_all | solution.py:118
  73.4 3.6 %copy-start.11 = (f32[2,16]{1,0:T(2,128)S(1)}, f32[2,16]{1,0:T(2,128)}, u32[]{:S(2)}) copy-start(f32[2,16]{1,0:T(2,128)} %param.26) | copy-start | bytes 388
  73.4 3.6 %copy-start.12 = (f32[2,16]{1,0:T(2,128)S(1)}, f32[2,16]{1,0:T(2,128)}, u32[]{:S(2)}) copy-start(f32[2,16]{1,0:T(2,128)} %param.27) | copy-start | bytes 388
  76.9 0.7 copy-start.10

commit v3 on v2

--- a/solution.py
+++ b/solution.py
@@ -1,6 +1,8 @@
 import jax
 import jax.numpy as jnp
 from jax import lax
+from jax.experimental import pallas as pl
+from jax.experimental.pallas import tpu as pltpu
 from jax.sharding import PartitionSpec as P
 
 MB = 4
@@ -30,6 +32,40 @@
 
 def mean_block(matrix):
     return jnp.sum(matrix.astype(jnp.float32), axis=0) * (1.0 / MB)
+
+
+def means_kernel(*refs):
+    count = (len(refs) - 1) // 2
+    grads, means, square_ref = refs[:count], refs[count : 2 * count], refs[2 * count]
+    lanes = square_ref.shape[-1]
+    square = jnp.zeros((grads[0].shape[1], lanes), jnp.float32)
+    for grad_ref, mean_ref in zip(grads, means):
+        total = grad_ref[0].astype(jnp.float32)
+        for batch in range(1, grad_ref.shape[0]):
+            total = total + grad_ref[batch].astype(jnp.float32)
+        averaged = total * (1.0 / MB)
+        mean_ref[...] = averaged
+        for start in range(0, averaged.shape[1], lanes):
+            part = averaged[:, start : start + lanes]
+            square = square + part * part
+    square_ref[...] = jnp.sum(square, axis=0, keepdims=True)
+
+
+def means_and_squares(blocks, lanes):
+    rows = blocks[0].shape[1]
+    out_shape = [jax.ShapeDtypeStruct((rows, matrix.shape[2]), jnp.float32) for matrix in blocks]
+    out_shape.append(jax.ShapeDtypeStruct((1, lanes), jnp.float32))
+    read = sum(matrix.size * matrix.dtype.itemsize for matrix in blocks)
+    outs = pl.pallas_call(
+        means_kernel,
+        out_shape=out_shape,
+        in_specs=[pl.BlockSpec(memory_space=pltpu.VMEM)] * len(blocks),
+        out_specs=[pl.BlockSpec(memory_space=pltpu.VMEM)] * len(out_shape),
+        cost_estimate=pl.CostEstimate(
+            flops=3 * sum(matrix.size for matrix in blocks), transcendentals=0, bytes_accessed=3 * read
+        ),
+    )(*blocks)
+    return list(outs[:-1]), outs[-1].reshape(lanes)
 
 
 def by_destination(group_means, shard_count):
@@ -77,11 +113,8 @@
     group_widths = [matrix.shape[2] // shard_count for matrix in blocks]
     flat_width = sum(group_widths)
 
-    group_means = [mean_block(matrix) for matrix in blocks]
     lanes = 128
-    block_square = jnp.sum((group_means[0] * group_means[0]).reshape(-1, lanes), axis=0)
-    for averaged in group_means[1:]:
-        block_square = block_square + jnp.sum((averaged * averaged).reshape(-1, lanes), axis=0)
+    group_means, block_square = means_and_squares(blocks, lanes)
 
     gain_local = jnp.sum(grad_norms.astype(jnp.float32), axis=(0, 1))
     gain_size = gain_local.size

time: 97.8 us -> 99.2 us (1.014)
  Pallas kernels: 0 us -> 1.98 us
    mul x21 -> x0, local copies, waits for them, and re-layouts: 5.14 us -> none  [the longest x14 5.1 us: mean_block(): return jnp.sum(matrix.astype(jnp.float32), axis=0) * (1.0 / MB)]
    reshape x0 -> x10, local copies, waits for them, and re-layouts: none -> 4.46 us  [by_destination(): matrix.reshape(rows, shard_count, matrix.shape[-1] // shard_count)]
    pallas_call x0 -> x1, Pallas kernels: none -> 1.98 us  [means_and_squares(): pl.pallas_call(means_kernel, out_shape=out_shape, in_specs=[pl.BlockSpec(...]
    reduce_sum x14 -> x0, other arithmetic: 1.25 us -> none  [the longest x7 1.04 us: mean_block(): return jnp.sum(matrix.astype(jnp.float32), axis=0) * (1.0 / MB)]
    pallas_call x0 -> x4, local copies, waits for them, and re-layouts: none -> 1.24 us  [means_and_squares(): pl.pallas_call(means_kernel, out_shape=out_shape, in_specs=[pl.BlockSpec(...]
  transfers between devices with their start and end apart: 4 -> 4, of which waited for: 3 -> 3; matrix products, arithmetic and copies ran while one was open for 16% -> 17% of each run, Pallas kernels for 0% -> 0%
where the time goes in v3:
time: 99.2 us; the launch traced here: 98.3 us
  starting transfers between devices  32.4 us (33%)
  local copies, waits for them, and re-layouts  27.9 us (28%)
  waiting for transfers between devices  22 us (22%)
  other arithmetic  11 us (11%)
  between operations  2.92 us (3%)
  Pallas kernels  1.98 us (2%)
    all_to_all x1, starting transfers between devices, shards(): lax.all_to_all(payload, 'shard', split_axis=0, concat_axis=0, tiled=True)  19.1 us
    all_to_all x1, waiting for transfers between devices, shards(): lax.all_to_all(payload, 'shard', split_axis=0, concat_axis=0, tiled=True)  11.9 us
    unnamed x40, local copies, waits for them, and re-layouts  10.6 us
    all_to_all x1, waiting for transfers between devices, shards(): lax.all_to_all(lowered, 'shard', split_axis=0, concat_axis=0, tiled=True)  8.51 us
    ppermute x2, starting transfers between devices, tensor_sum(): value = value + lax.ppermute(value, 'tensor', pairs)  7.64 us
    all_to_all x1, starting transfers between devices, shards(): lax.all_to_all(lowered, 'shard', split_axis=0, concat_axis=0, tiled=True)  5.65 us
    reshape x10, local copies, waits for them, and re-layouts, by_destination(): matrix.reshape(rows, shard_count, matrix.shape[-1] // shard_count)  4.46 us
    reshape x3, local copies, waits for them, and re-layouts, shards(): jnp.transpose(section, (1, 0, 2)).reshape(rows, shard_count * group_width)  3.86 us
  transfers between devices with their start and end apart: 4, of which 3 were waited for; matrix products, arithmetic and copies ran while one was open for 17% of the time, Pallas kernels for 0%

profile of v3, /device:TPU:1, one launch (start us, length us, event | category | flops | bytes accessed | tf_op | source)
XLA Modules:
  0.0 98.3 jit_solution(11605759238945263347)
XLA Ops:
  0.6 0.7 convert_reduce_fusion
  1.4 2.0 %shard_map.253 = (f32[16,512]{1,0:T(8,128)}, f32[16,512]{1,0:T(8,128)}, f32[16,512]{1,0:T(8,128)}, f32[16,512]{1,0:T(8,128)}, f32[16,1280]{1,0:T(8,128)}, /*inde...) custom-call(bf16[4,16,512]{2,1,0:T(8,128)(2,1)} %refs_0_.1, bf16[4,16,512]{2,1,0:T(8,128)(2,1)} %refs_1_.1, ...), custom_call_target="tpu_custom_call" | custom-call | flops 1130496 | bytes 2260992 | tf_op jit(solution)/shard_map/pallas_call | solution.py:59
  4.1 3.9 %collective-permute-start = (f32[160]{0:T(256)S(1)}, f32[160]{0:T(256)S(1)}, u32[]{:S(2)}, u32[]{:S(2)}) collective-permute-start(f32[160]{0:T(256)S(1)} %pad_maximum_fusion), channel_id=1, source_target_pairs={{0,1},{1,0},{2,3},{3,2},{4,5},{5,4},{6,7},{7,6},{8,9},{9,8},{10,11... | collective-permute-start | bytes 1928 | tf_op jit(solution)/shard_map/ppermute | solution.py:90
  8.1 0.9 copy.80
  9.1 0.8 copy-done.8
  11.0 0.7 copy-done.6
  11.8 0.8 copy-done.5
  12.6 1.0 %reshape.152 = f32[16,128,10]{2,1,0:T(8,128)S(1)} reshape(f32[16,1280]{1,0:T(8,128)S(1)} %copy-done.5) | data formatting | bytes 163840 | tf_op jit(solution)/shard_map/reshape | solution.py:74
  14.6 1.0 %reshape.153 = f32[16,128,10]{2,1,0:T(8,128)S(1)} reshape(f32[16,1280]{1,0:T(8,128)S(1)} %copy-done.4) | data formatting | bytes 163840 | tf_op jit(solution)/shard_map/reshape | solution.py:74
  16.1 0.9 copy-done.3
  16.9 1.0 %reshape.154 = f32[16,128,10]{2,1,0:T(8,128)S(1)} reshape(f32[16,1280]{1,0:T(8,128)S(1)} %copy-done.3) | data formatting | bytes 163840 | tf_op jit(solution)/shard_map/reshape | solution.py:74
  18.4 3.7 %collective-permute-start.1 = (f32[160]{0:T(256)S(1)}, f32[160]{0:T(256)S(1)}, u32[]{:S(2)}, u32[]{:S(2)}) collective-permute-start(f32[160]{0:T(256)S(1)} %fusion.9), channel_id=1, source_target_pairs={{0,3},{1,2},{2,1},{3,0},{4,7},{5,6},{6,5},{7,4},{8,11},{9,10},{10,... | collective-permute-start | bytes 1928 | tf_op jit(solution)/shard_map/ppermute | solution.py:90
  22.3 1.6 %collective-permute-done.1 = f32[160]{0:T(256)S(1)} collective-permute-done((f32[160]{0:T(256)S(1)}, f32[160]{0:T(256)S(1)}, u32[]{:S(2)}, u32[]{:S(2)}) %collective-permute-start.1) | collective-permute-done | bytes 672 | tf_op jit(solution)/shard_map/ppermute | solution.py:90
  23.9 0.7 add_reduce_fusion
  24.6 0.7 pad_bitcast_fusion
  25.3 1.3 %copy.92 = f32[128,1,737]{2,1,0:T(1,128)} copy(f32[128,1,737]{0,2,1:T(8,128)S(1)} %pad_bitcast_fusion) | data formatting | bytes 754688 | tf_op jit(solution)/shard_map/all_to_all | solution.py:132
  26.6 19.1 %all-to-all-start = ((f32[128,1,737]{2,1,0:T(1,128)}), f32[128,1,737]{2,1,0:T(1,128)S(1)}, u32[]{:S(2)}, u32[]{:S(2)}) async-start(f32[128,1,737]{2,1,0:T(1,128)} %copy.92), calls=%async_computation | async-start | bytes 786432 | tf_op jit(solution)/shard_map/all_to_all | solution.py:132
  45.8 2.3 %multiply_reduce_fusion = (f32[94208]{0:T(1024)S(1)}, f32[94208]{0:T(1024)S(1)}) fusion(f32[1,1,94208]{2,1,0:T(1,128)S(1)} %copy-done.1, f32[1,1,94208]{2,1,0:T(1,128)S(1)} %copy-done.2), kind=kLoop, calls=%fused_computation.14 | loop fusion | flops 188416 | bytes 1507328 | tf_op jit(solution)/shard_map/mul | solution.py:24
  49.7 1.5 %reduce.12 = f32[94208]{0:T(1024)S(1)} reduce(f32[1,1,94208]{2,1,0:T(1,128)S(1)} %copy-done, f32[]{:T(128)} %broadcast.75), dimensions={0,1}, to_apply=%param.22.reduce_sub_computation.3 | reduce | bytes 753668 | tf_op args[8]
  51.7 11.9 %all-to-all-done = f32[128,1,737]{2,1,0:T(1,128)S(1)} async-done(((f32[128,1,737]{2,1,0:T(1,128)}), f32[128,1,737]{2,1,0:T(1,128)S(1)}, u32[]{:S(2)}, u32[]{:S(2)}) %all-to-all-start) | async-done | bytes 377376 | tf_op jit(solution)/shard_map/all_to_all | solution.py:132
  66.4 0.7 reduce.13
  67.3 0.9 reshape.186
  68.2 5.6 %all-to-all-start.1 = ((bf16[128,2,368]{2,1,0:T(2,128)(2,1)}), bf16[128,2,368]{2,1,0:T(2,128)(2,1)S(1)}, u32[]{:S(2)}, u32[]{:S(2)}) async-start(bf16[128,2,368]{2,1,0:T(2,128)(2,1)} %reshape.186), calls=%async_computation.1 | async-start | bytes 393216 | tf_op jit(solution)/shard_map/all_to_all | solution.py:151
  74.6 3.5 %multiply_subtract_fusion = (f32[1,1,94208]{2,1,0:T(1,128)}, f32[1,1,94208]{2,1,0:T(1,128)}, f32[1,1,94208]{2,1,0:T(1,128)}) fusion(f32[1,1,94208]{2,1,0:T(1,128)S(1)} %copy-done, f32[1,1,94208]{2,1,0:T(1,128)S(1)} %mul.190, f32[1,1,94208]{2,1,0:T(1,128)S(1)} %copy-done.2, f32[1,1,94208]{2,1,0:T(1,128)S(1)} %copy-done.1), kind=kLoop, calls=%fused_computation.12 | loop fusion | flops 1413120 | bytes 2637824 | tf_op jit(solution)/shard_map/sub | solution.py:30
  79.4 8.5 %all-to-all-done.1 = bf16[128,2,368]{2,1,0:T(2,128)(2,1)S(1)} async-done(((bf16[128,2,368]{2,1,0:T(2,128)(2,1)}), bf16[128,2,368]{2,1,0:T(2,128)(2,1)S(1)}, u32[]{:S(2)}, u32[]{:S(2)}) %all-to-all-start.1) | async-done | bytes 188448 | tf_op jit(solution)/shard_map/all_to_all | solution.py:151
  89.4 1.3 %reshape.164 = bf16[16,1280]{1,0:T(8,128)(2,1)} reshape(bf16[16,128,10]{2,1,0:T(8,128)(2,1)S(1)} %copy.105) | data formatting | bytes 81920 | tf_op jit(solution)/shard_map/reshape | solution.py:157
  91.0 1.3 %reshape.165 = bf16[16,1280]{1,0:T(8,128)(2,1)} reshape(bf16[16,128,10]{2,1,0:T(8,128)(2,1)S(1)} %copy.106) | data formatting | bytes 81920 | tf_op jit(solution)/shard_map/reshape | solution.py:157
  92.6 1.3 %reshape.166 = bf16[16,1280]{1,0:T(8,128)(2,1)} reshape(bf16[16,128,10]{2,1,0:T(8,128)(2,1)S(1)} %copy.107) | data formatting | bytes 81920 | tf_op jit(solution)/shard_map/reshape | solution.py:157
  94.0 0.7 copy.108
  94.8 0.7 copy.109
  95.7 0.7 copy.110
  96.5 0.7 copy.111
  (76 shorter events, 13.0 us)
Async XLA Ops:
  3.4 0.7 copy-start.9
  4.1 14.2 %collective-permute-start = (f32[160]{0:T(256)S(1)}, f32[160]{0:T(256)S(1)}, u32[]{:S(2)}, u32[]{:S(2)}) collective-permute-start(f32[160]{0:T(256)S(1)} %pad_maximum_fusion), channel_id=1, source_target_pairs={{0,1},{1,0},{2,3},{3,2},{4,5},{5,4},{6,7},{7,6},{8,9},{9,8},{10,11... | collective-permute-start | bytes 1928 | tf_op jit(solution)/shard_map/ppermute | solution.py:90
  9.0 0.8 copy-start.8
  10.0 0.8 copy-start.7
  10.9 0.8 copy-start.6
  11.7 0.9 copy-start.5
  13.7 0.9 copy-start.4
  16.0 0.9 copy-start.3
  18.4 5.5 %collective-permute-start.1 = (f32[160]{0:T(256)S(1)}, f32[160]{0:T(256)S(1)}, u32[]{:S(2)}, u32[]{:S(2)}) collective-permute-start(f32[160]{0:T(256)S(1)} %fusion.9), channel_id=1, source_target_pairs={{0,3},{1,2},{2,1},{3,0},{4,7},{5,6},{6,5},{7,4},{8,11},{9,10},{10,... | collective-permute-start | bytes 1928 | tf_op jit(solution)/shard_map/ppermute | solution.py:90
  26.6 19.2 %copy-start.1 = (f32[1,1,94208]{2,1,0:T(1,128)S(1)}, f32[1,1,94208]{2,1,0:T(1,128)}, u32[]{:S(2)}) copy-start(f32[1,1,94208]{2,1,0:T(1,128)} %param.24) | copy-start | bytes 1130500
  26.6 19.2 %copy-start.2 = (f32[1,1,94208]{2,1,0:T(1,128)S(1)}, f32[1,1,94208]{2,1,0:T(1,128)}, u32[]{:S(2)}) copy-start(f32[1,1,94208]{2,1,0:T(1,128)} %param.23) | copy-start | bytes 1130500
  26.6 37.0 %all-to-all-start = ((f32[128,1,737]{2,1,0:T(1,128)}), f32[128,1,737]{2,1,0:T(1,128)S(1)}, u32[]{:S(2)}, u32[]{:S(2)}) async-start(f32[128,1,737]{2,1,0:T(1,128)} %copy.92), calls=%async_computation | async-start | bytes 786432 | tf_op jit(solution)/shard_map/all_to_all | solution.py:132
  48.7 1.0 %copy-start = (f32[1,1,94208]{2,1,0:T(1,128)S(1)}, f32[1,1,94208]{2,1,0:T(1,128)}, u32[]{:S(2)}) copy-start(f32[1,1,94208]{2,1,0:T(1,128)} %param.22) | copy-start | bytes 1130500
  68.2 19.7 %all-to-all-start.1 = ((bf16[128,2,368]{2,1,0:T(2,128)(2,1)}), bf16[128,2,368]{2,1,0:T(2,128)(2,1)S(1)}, u32[]{:S(2)}, u32[]{:S(2)}) async-start(bf16[128,2,368]{2,1,0:T(2,128)(2,1)} %reshape.186), calls=%async_computation.1 | async-start | bytes 393216 | tf_op jit(solution)/shard_map/all_to_all | solution.py:151
  74.6 3.6 %copy-start.11 = (f32[2,16]{1,0:T(2,128)S(1)}, f32[2,16]{1,0:T(2,128)}, u32[]{:S(2)}) copy-start(f32[2,16]{1,0:T(2,128)} %param.26) | copy-start | bytes 388
  74.6 3.6 %copy-start.12 = (f32[2,16]{1,0:T(2,128)S(1)}, f32[2,16]{1,0:T(2,128)}, u32[]{:S(2)}) copy-start(f32[2,16]{1,0:T(2,128)} %param.27) | copy-start | bytes 388
  78.1 0.7 copy-start.10

commit v4 on v2

--- a/solution.py
+++ b/solution.py
@@ -43,16 +43,16 @@
 
 def tensor_sum(value):
     count = lax.axis_size("tensor")
-    if count == 4:
-        masks = (1, 3)
-    elif count & (count - 1) == 0:
-        masks = tuple(1 << bit for bit in range(count.bit_length() - 1))
-    else:
-        return lax.psum(value, "tensor")
-    for mask in masks:
-        pairs = [(index, index ^ mask) for index in range(count)]
-        value = value + lax.ppermute(value, "tensor", pairs)
-    return value
+    index = lax.axis_index("tensor")
+    parts = [value]
+    for shift in range(1, count):
+        pairs = [(source, (source - shift) % count) for source in range(count)]
+        parts.append(lax.ppermute(value, "tensor", pairs))
+    by_source = jnp.roll(jnp.stack(parts), index, axis=0)
+    total = by_source[0]
+    for source in range(1, count):
+        total = total + by_source[source]
+    return total
 
 
 def shards(

time: 97.8 us -> 98.1 us (level)
  starting transfers between devices: 32.4 us -> 34.3 us
  waiting for transfers between devices: 22 us -> 20.4 us
    ppermute x2 -> x3, starting transfers between devices: 7.64 us -> 10.1 us  [tensor_sum(): parts.append(lax.ppermute(value, 'tensor', pairs))]
    ppermute x2 -> x3, waiting for transfers between devices: 1.62 us -> 0.01 us  [tensor_sum(): parts.append(lax.ppermute(value, 'tensor', pairs))]
  transfers between devices with their start and end apart: 4 -> 5, of which waited for: 3 -> 2; matrix products, arithmetic and copies ran while one was open for 16% -> 16% of each run, Pallas kernels for 0% -> 0%
where the time goes in v4:
time: 98.1 us; the launch traced here: 97.5 us
  starting transfers between devices  34.3 us (35%)
  local copies, waits for them, and re-layouts  27.9 us (28%)
  waiting for transfers between devices  20.4 us (21%)
  other arithmetic  11.6 us (12%)
  between operations  3.13 us (3%)
    all_to_all x1, starting transfers between devices, shards(): lax.all_to_all(payload, 'shard', split_axis=0, concat_axis=0, tiled=True)  18.6 us
    all_to_all x1, waiting for transfers between devices, shards(): lax.all_to_all(payload, 'shard', split_axis=0, concat_axis=0, tiled=True)  11.9 us
    unnamed x40, local copies, waits for them, and re-layouts  11.1 us
    ppermute x3, starting transfers between devices, tensor_sum(): parts.append(lax.ppermute(value, 'tensor', pairs))  10.1 us
    all_to_all x1, waiting for transfers between devices, shards(): lax.all_to_all(lowered, 'shard', split_axis=0, concat_axis=0, tiled=True)  8.49 us
    all_to_all x1, starting transfers between devices, shards(): lax.all_to_all(lowered, 'shard', split_axis=0, concat_axis=0, tiled=True)  5.64 us
    mul x14, local copies, waits for them, and re-layouts, mean_block(): return jnp.sum(matrix.astype(jnp.float32), axis=0) * (1.0 / MB)  5.13 us
    reshape x3, local copies, waits for them, and re-layouts, shards(): jnp.transpose(section, (1, 0, 2)).reshape(rows, shard_count * group_width)  3.86 us
  transfers between devices with their start and end apart: 5, of which 2 were waited for; matrix products, arithmetic and copies ran while one was open for 16% of the time, Pallas kernels for 0%

profile of v4, /device:TPU:1, one launch (start us, length us, event | category | flops | bytes accessed | tf_op | source)
XLA Modules:
  0.0 97.5 jit_solution(12730771251678468639)
XLA Ops:
  0.6 0.9 convert_reduce_fusion.2
  1.6 0.9 copy-done.3
  2.7 0.8 copy-done.4
  3.6 0.8 copy-done.5
  4.5 0.8 copy-done.6
  5.3 0.8 copy-done.7
  6.2 0.8 copy-done.8
  7.9 5.2 %collective-permute-start = (f32[160]{0:T(256)S(1)}, f32[160]{0:T(256)S(1)}, u32[]{:S(2)}, u32[]{:S(2)}) collective-permute-start(f32[160]{0:T(256)S(1)} %pad_maximum_fusion), channel_id=1, source_target_pairs={{0,3},{1,0},{2,1},{3,2},{4,7},{5,4},{6,5},{7,6},{8,11},{9,8},{10,9... | collective-permute-start | bytes 1928 | tf_op jit(solution)/shard_map/ppermute | solution.py:50
  13.1 2.4 %collective-permute-start.1 = (f32[160]{0:T(256)S(1)}, f32[160]{0:T(256)S(1)}, u32[]{:S(2)}, u32[]{:S(2)}) collective-permute-start(f32[160]{0:T(256)S(1)} %pad_maximum_fusion), channel_id=1, source_target_pairs={{0,2},{1,3},{2,0},{3,1},{4,6},{5,7},{6,4},{7,5},{8,10},{9,11},{10,... | collective-permute-start | bytes 1928 | tf_op jit(solution)/shard_map/ppermute | solution.py:50
  15.6 2.5 %collective-permute-start.2 = (f32[160]{0:T(256)S(1)}, f32[160]{0:T(256)S(1)}, u32[]{:S(2)}, u32[]{:S(2)}) collective-permute-start(f32[160]{0:T(256)S(1)} %pad_maximum_fusion), channel_id=1, source_target_pairs={{0,1},{1,2},{2,3},{3,0},{4,5},{5,6},{6,7},{7,4},{8,9},{9,10},{10,1... | collective-permute-start | bytes 1928 | tf_op jit(solution)/shard_map/ppermute | solution.py:50
  19.1 1.1 %mul.307 = f32[16,128,10]{2,1,0:T(8,128)S(1)} reshape(f32[16,1280]{1,0:T(8,128)S(1)} %get-tuple-element.92) | data formatting | bytes 163840 | tf_op jit(solution)/shard_map/mul | solution.py:32
  20.5 1.1 %mul.309 = f32[16,128,10]{2,1,0:T(8,128)S(1)} reshape(f32[16,1280]{1,0:T(8,128)S(1)} %get-tuple-element.94) | data formatting | bytes 163840 | tf_op jit(solution)/shard_map/mul | solution.py:32
  21.9 1.1 %mul.311 = f32[16,128,10]{2,1,0:T(8,128)S(1)} reshape(f32[16,1280]{1,0:T(8,128)S(1)} %get-tuple-element.96) | data formatting | bytes 163840 | tf_op jit(solution)/shard_map/mul | solution.py:32
  23.6 0.7 fusion.10
  24.3 0.7 pad_bitcast_fusion
  25.0 1.3 %copy.113 = f32[128,1,737]{2,1,0:T(1,128)} copy(f32[128,1,737]{0,2,1:T(8,128)S(1)} %pad_bitcast_fusion) | data formatting | bytes 754688 | tf_op jit(solution)/shard_map/all_to_all | solution.py:99
  26.3 18.6 %all-to-all-start = ((f32[128,1,737]{2,1,0:T(1,128)}), f32[128,1,737]{2,1,0:T(1,128)S(1)}, u32[]{:S(2)}, u32[]{:S(2)}) async-start(f32[128,1,737]{2,1,0:T(1,128)} %copy.113), calls=%async_computation | async-start | bytes 786432 | tf_op jit(solution)/shard_map/all_to_all | solution.py:99
  44.9 2.3 %multiply_reduce_fusion = (f32[94208]{0:T(1024)S(1)}, f32[94208]{0:T(1024)S(1)}) fusion(f32[1,1,94208]{2,1,0:T(1,128)S(1)} %copy-done.1, f32[1,1,94208]{2,1,0:T(1,128)S(1)} %copy-done.2), kind=kLoop, calls=%fused_computation.17 | loop fusion | flops 188416 | bytes 1507328 | tf_op jit(solution)/shard_map/mul | solution.py:22
  48.8 1.5 %reduce.16 = f32[94208]{0:T(1024)S(1)} reduce(f32[1,1,94208]{2,1,0:T(1,128)S(1)} %copy-done, f32[]{:T(128)} %broadcast.140), dimensions={0,1}, to_apply=%param.22.reduce_sub_computation.3 | reduce | bytes 753668 | tf_op args[8]
  50.8 11.9 %all-to-all-done = f32[128,1,737]{2,1,0:T(1,128)S(1)} async-done(((f32[128,1,737]{2,1,0:T(1,128)}), f32[128,1,737]{2,1,0:T(1,128)S(1)}, u32[]{:S(2)}, u32[]{:S(2)}) %all-to-all-start) | async-done | bytes 377376 | tf_op jit(solution)/shard_map/all_to_all | solution.py:99
  65.5 0.7 reduce.17
  66.4 0.9 reshape.230
  67.3 5.6 %all-to-all-start.1 = ((bf16[128,2,368]{2,1,0:T(2,128)(2,1)}), bf16[128,2,368]{2,1,0:T(2,128)(2,1)S(1)}, u32[]{:S(2)}, u32[]{:S(2)}) async-start(bf16[128,2,368]{2,1,0:T(2,128)(2,1)} %reshape.230), calls=%async_computation.1 | async-start | bytes 393216 | tf_op jit(solution)/shard_map/all_to_all | solution.py:118
  73.7 3.5 %multiply_subtract_fusion = (f32[1,1,94208]{2,1,0:T(1,128)}, f32[1,1,94208]{2,1,0:T(1,128)}, f32[1,1,94208]{2,1,0:T(1,128)}) fusion(f32[1,1,94208]{2,1,0:T(1,128)S(1)} %copy-done, f32[1,1,94208]{2,1,0:T(1,128)S(1)} %mul.332, f32[1,1,94208]{2,1,0:T(1,128)S(1)} %copy-done.2, f32[1,1,94208]{2,1,0:T(1,128)S(1)} %copy-done.1), kind=kLoop, calls=%fused_computation.12 | loop fusion | flops 1413120 | bytes 2637824 | tf_op jit(solution)/shard_map/sub | solution.py:28
  78.5 8.5 %all-to-all-done.1 = bf16[128,2,368]{2,1,0:T(2,128)(2,1)S(1)} async-done(((bf16[128,2,368]{2,1,0:T(2,128)(2,1)}), bf16[128,2,368]{2,1,0:T(2,128)(2,1)S(1)}, u32[]{:S(2)}, u32[]{:S(2)}) %all-to-all-start.1) | async-done | bytes 188448 | tf_op jit(solution)/shard_map/all_to_all | solution.py:118
  88.5 1.3 %reshape.201 = bf16[16,1280]{1,0:T(8,128)(2,1)} reshape(bf16[16,128,10]{2,1,0:T(8,128)(2,1)S(1)} %copy.126) | data formatting | bytes 81920 | tf_op jit(solution)/shard_map/reshape | solution.py:124
  90.1 1.3 %reshape.202 = bf16[16,1280]{1,0:T(8,128)(2,1)} reshape(bf16[16,128,10]{2,1,0:T(8,128)(2,1)S(1)} %copy.127) | data formatting | bytes 81920 | tf_op jit(solution)/shard_map/reshape | solution.py:124
  91.7 1.3 %reshape.203 = bf16[16,1280]{1,0:T(8,128)(2,1)} reshape(bf16[16,128,10]{2,1,0:T(8,128)(2,1)S(1)} %copy.128) | data formatting | bytes 81920 | tf_op jit(solution)/shard_map/reshape | solution.py:124
  93.1 0.7 copy.129
  93.9 0.7 copy.130
  94.8 0.7 copy.131
  95.6 0.7 copy.132
  (106 shorter events, 12.4 us)
Async XLA Ops:
  1.6 0.9 copy-start.3
  2.6 0.9 copy-start.4
  3.5 0.8 copy-start.5
  4.4 0.8 copy-start.6
  5.3 0.8 copy-start.7
  6.2 0.8 copy-start.8
  7.0 0.7 copy-start.9
  7.9 15.6 %collective-permute-start = (f32[160]{0:T(256)S(1)}, f32[160]{0:T(256)S(1)}, u32[]{:S(2)}, u32[]{:S(2)}) collective-permute-start(f32[160]{0:T(256)S(1)} %pad_maximum_fusion), channel_id=1, source_target_pairs={{0,3},{1,0},{2,1},{3,2},{4,7},{5,4},{6,5},{7,6},{8,11},{9,8},{10,9... | collective-permute-start | bytes 1928 | tf_op jit(solution)/shard_map/ppermute | solution.py:50
  13.1 10.4 %collective-permute-start.1 = (f32[160]{0:T(256)S(1)}, f32[160]{0:T(256)S(1)}, u32[]{:S(2)}, u32[]{:S(2)}) collective-permute-start(f32[160]{0:T(256)S(1)} %pad_maximum_fusion), channel_id=1, source_target_pairs={{0,2},{1,3},{2,0},{3,1},{4,6},{5,7},{6,4},{7,5},{8,10},{9,11},{10,... | collective-permute-start | bytes 1928 | tf_op jit(solution)/shard_map/ppermute | solution.py:50
  15.6 8.0 %collective-permute-start.2 = (f32[160]{0:T(256)S(1)}, f32[160]{0:T(256)S(1)}, u32[]{:S(2)}, u32[]{:S(2)}) collective-permute-start(f32[160]{0:T(256)S(1)} %pad_maximum_fusion), channel_id=1, source_target_pairs={{0,1},{1,2},{2,3},{3,0},{4,5},{5,6},{6,7},{7,4},{8,9},{9,10},{10,1... | collective-permute-start | bytes 1928 | tf_op jit(solution)/shard_map/ppermute | solution.py:50
  26.3 18.6 %copy-start.1 = (f32[1,1,94208]{2,1,0:T(1,128)S(1)}, f32[1,1,94208]{2,1,0:T(1,128)}, u32[]{:S(2)}) copy-start(f32[1,1,94208]{2,1,0:T(1,128)} %param.24) | copy-start | bytes 1130500
  26.3 18.6 %copy-start.2 = (f32[1,1,94208]{2,1,0:T(1,128)S(1)}, f32[1,1,94208]{2,1,0:T(1,128)}, u32[]{:S(2)}) copy-start(f32[1,1,94208]{2,1,0:T(1,128)} %param.23) | copy-start | bytes 1130500
  26.3 36.4 %all-to-all-start = ((f32[128,1,737]{2,1,0:T(1,128)}), f32[128,1,737]{2,1,0:T(1,128)S(1)}, u32[]{:S(2)}, u32[]{:S(2)}) async-start(f32[128,1,737]{2,1,0:T(1,128)} %copy.113), calls=%async_computation | async-start | bytes 786432 | tf_op jit(solution)/shard_map/all_to_all | solution.py:99
  47.8 1.0 %copy-start = (f32[1,1,94208]{2,1,0:T(1,128)S(1)}, f32[1,1,94208]{2,1,0:T(1,128)}, u32[]{:S(2)}) copy-start(f32[1,1,94208]{2,1,0:T(1,128)} %param.22) | copy-start | bytes 1130500
  67.3 19.7 %all-to-all-start.1 = ((bf16[128,2,368]{2,1,0:T(2,128)(2,1)}), bf16[128,2,368]{2,1,0:T(2,128)(2,1)S(1)}, u32[]{:S(2)}, u32[]{:S(2)}) async-start(bf16[128,2,368]{2,1,0:T(2,128)(2,1)} %reshape.230), calls=%async_computation.1 | async-start | bytes 393216 | tf_op jit(solution)/shard_map/all_to_all | solution.py:118
  73.7 3.6 %copy-start.11 = (f32[2,16]{1,0:T(2,128)S(1)}, f32[2,16]{1,0:T(2,128)}, u32[]{:S(2)}) copy-start(f32[2,16]{1,0:T(2,128)} %param.26) | copy-start | bytes 388
  73.7 3.6 %copy-start.12 = (f32[2,16]{1,0:T(2,128)S(1)}, f32[2,16]{1,0:T(2,128)}, u32[]{:S(2)}) copy-start(f32[2,16]{1,0:T(2,128)} %param.27) | copy-start | bytes 388
  77.3 0.7 copy-start.10

commit v5 on v3

--- a/solution.py
+++ b/solution.py
@@ -79,16 +79,16 @@
 
 def tensor_sum(value):
     count = lax.axis_size("tensor")
-    if count == 4:
-        masks = (1, 3)
-    elif count & (count - 1) == 0:
-        masks = tuple(1 << bit for bit in range(count.bit_length() - 1))
-    else:
-        return lax.psum(value, "tensor")
-    for mask in masks:
-        pairs = [(index, index ^ mask) for index in range(count)]
-        value = value + lax.ppermute(value, "tensor", pairs)
-    return value
+    index = lax.axis_index("tensor")
+    parts = [value]
+    for shift in range(1, count):
+        pairs = [(source, (source - shift) % count) for source in range(count)]
+        parts.append(lax.ppermute(value, "tensor", pairs))
+    by_source = jnp.roll(jnp.stack(parts), index, axis=0)
+    total = by_source[0]
+    for source in range(1, count):
+        total = total + by_source[source]
+    return total
 
 
 def shards(

time: 99.2 us -> 98.4 us (level)
  starting transfers between devices: 32.4 us -> 34.3 us
  local copies, waits for them, and re-layouts: 27.9 us -> 26.2 us
  waiting for transfers between devices: 22 us -> 20.4 us
    ppermute x2 -> x3, starting transfers between devices: 7.64 us -> 10.1 us  [tensor_sum(): parts.append(lax.ppermute(value, 'tensor', pairs))]
    ppermute x2 -> x3, waiting for transfers between devices: 1.62 us -> 0.01 us  [tensor_sum(): parts.append(lax.ppermute(value, 'tensor', pairs))]
  transfers between devices with their start and end apart: 4 -> 5, of which waited for: 3 -> 2; matrix products, arithmetic and copies ran while one was open for 17% -> 16% of each run, Pallas kernels for 0% -> 0%
where the time goes in v5:
time: 98.4 us; the launch traced here: 97.5 us
  starting transfers between devices  34.3 us (35%)
  local copies, waits for them, and re-layouts  26.2 us (27%)
  waiting for transfers between devices  20.4 us (21%)
  other arithmetic  11.7 us (12%)
  between operations  2.99 us (3%)
  Pallas kernels  1.98 us (2%)
    all_to_all x1, starting transfers between devices, shards(): lax.all_to_all(payload, 'shard', split_axis=0, concat_axis=0, tiled=True)  18.6 us
    all_to_all x1, waiting for transfers between devices, shards(): lax.all_to_all(payload, 'shard', split_axis=0, concat_axis=0, tiled=True)  11.9 us
    ppermute x3, starting transfers between devices, tensor_sum(): parts.append(lax.ppermute(value, 'tensor', pairs))  10.1 us
    unnamed x40, local copies, waits for them, and re-layouts  9.67 us
    all_to_all x1, waiting for transfers between devices, shards(): lax.all_to_all(lowered, 'shard', split_axis=0, concat_axis=0, tiled=True)  8.49 us
    all_to_all x1, starting transfers between devices, shards(): lax.all_to_all(lowered, 'shard', split_axis=0, concat_axis=0, tiled=True)  5.6 us
    reshape x10, local copies, waits for them, and re-layouts, by_destination(): matrix.reshape(rows, shard_count, matrix.shape[-1] // shard_count)  4.46 us
    reshape x3, local copies, waits for them, and re-layouts, shards(): jnp.transpose(section, (1, 0, 2)).reshape(rows, shard_count * group_width)  3.86 us
  transfers between devices with their start and end apart: 5, of which 2 were waited for; matrix products, arithmetic and copies ran while one was open for 16% of the time, Pallas kernels for 0%

profile of v5, /device:TPU:1, one launch (start us, length us, event | category | flops | bytes accessed | tf_op | source)
XLA Modules:
  0.0 97.5 jit_solution(2064501678346321653)
XLA Ops:
  0.6 0.7 convert_reduce_fusion
  1.4 2.0 %shard_map.253 = (f32[16,512]{1,0:T(8,128)}, f32[16,512]{1,0:T(8,128)}, f32[16,512]{1,0:T(8,128)}, f32[16,512]{1,0:T(8,128)}, f32[16,1280]{1,0:T(8,128)}, /*inde...) custom-call(bf16[4,16,512]{2,1,0:T(8,128)(2,1)} %refs_0_.1, bf16[4,16,512]{2,1,0:T(8,128)(2,1)} %refs_1_.1, ...), custom_call_target="tpu_custom_call" | custom-call | flops 1130496 | bytes 2260992 | tf_op jit(solution)/shard_map/pallas_call | solution.py:59
  3.4 0.7 pad_maximum_fusion
  4.1 5.2 %collective-permute-start = (f32[160]{0:T(256)S(1)}, f32[160]{0:T(256)S(1)}, u32[]{:S(2)}, u32[]{:S(2)}) collective-permute-start(f32[160]{0:T(256)S(1)} %pad_maximum_fusion), channel_id=1, source_target_pairs={{0,3},{1,0},{2,1},{3,2},{4,7},{5,4},{6,5},{7,6},{8,11},{9,8},{10,9... | collective-permute-start | bytes 1928 | tf_op jit(solution)/shard_map/ppermute | solution.py:86
  9.3 2.4 %collective-permute-start.1 = (f32[160]{0:T(256)S(1)}, f32[160]{0:T(256)S(1)}, u32[]{:S(2)}, u32[]{:S(2)}) collective-permute-start(f32[160]{0:T(256)S(1)} %pad_maximum_fusion), channel_id=1, source_target_pairs={{0,2},{1,3},{2,0},{3,1},{4,6},{5,7},{6,4},{7,5},{8,10},{9,11},{10,... | collective-permute-start | bytes 1928 | tf_op jit(solution)/shard_map/ppermute | solution.py:86
  11.8 2.5 %collective-permute-start.2 = (f32[160]{0:T(256)S(1)}, f32[160]{0:T(256)S(1)}, u32[]{:S(2)}, u32[]{:S(2)}) collective-permute-start(f32[160]{0:T(256)S(1)} %pad_maximum_fusion), channel_id=1, source_target_pairs={{0,1},{1,2},{2,3},{3,0},{4,5},{5,6},{6,7},{7,4},{8,9},{9,10},{10,1... | collective-permute-start | bytes 1928 | tf_op jit(solution)/shard_map/ppermute | solution.py:86
  14.6 0.8 copy-done.8
  15.6 0.7 copy-done.7
  16.4 0.7 copy-done.6
  17.3 0.8 copy-done.5
  18.1 1.0 %reshape.157 = f32[16,128,10]{2,1,0:T(8,128)S(1)} reshape(f32[16,1280]{1,0:T(8,128)S(1)} %copy-done.5) | data formatting | bytes 163840 | tf_op jit(solution)/shard_map/reshape | solution.py:74
  20.1 1.0 %reshape.158 = f32[16,128,10]{2,1,0:T(8,128)S(1)} reshape(f32[16,1280]{1,0:T(8,128)S(1)} %copy-done.4) | data formatting | bytes 163840 | tf_op jit(solution)/shard_map/reshape | solution.py:74
  22.0 1.0 %reshape.159 = f32[16,128,10]{2,1,0:T(8,128)S(1)} reshape(f32[16,1280]{1,0:T(8,128)S(1)} %copy-done.3) | data formatting | bytes 163840 | tf_op jit(solution)/shard_map/reshape | solution.py:74
  23.8 0.7 fusion.10
  24.5 0.7 pad_bitcast_fusion
  25.1 1.3 %copy.92 = f32[128,1,737]{2,1,0:T(1,128)} copy(f32[128,1,737]{0,2,1:T(8,128)S(1)} %pad_bitcast_fusion) | data formatting | bytes 754688 | tf_op jit(solution)/shard_map/all_to_all | solution.py:132
  26.4 18.6 %all-to-all-start = ((f32[128,1,737]{2,1,0:T(1,128)}), f32[128,1,737]{2,1,0:T(1,128)S(1)}, u32[]{:S(2)}, u32[]{:S(2)}) async-start(f32[128,1,737]{2,1,0:T(1,128)} %copy.92), calls=%async_computation | async-start | bytes 786432 | tf_op jit(solution)/shard_map/all_to_all | solution.py:132
  45.0 2.3 %multiply_reduce_fusion = (f32[94208]{0:T(1024)S(1)}, f32[94208]{0:T(1024)S(1)}) fusion(f32[1,1,94208]{2,1,0:T(1,128)S(1)} %copy-done.1, f32[1,1,94208]{2,1,0:T(1,128)S(1)} %copy-done.2), kind=kLoop, calls=%fused_computation.14 | loop fusion | flops 188416 | bytes 1507328 | tf_op jit(solution)/shard_map/mul | solution.py:24
  49.0 1.5 %reduce.16 = f32[94208]{0:T(1024)S(1)} reduce(f32[1,1,94208]{2,1,0:T(1,128)S(1)} %copy-done, f32[]{:T(128)} %broadcast.79), dimensions={0,1}, to_apply=%param.22.reduce_sub_computation.3 | reduce | bytes 753668 | tf_op args[8]
  50.9 11.9 %all-to-all-done = f32[128,1,737]{2,1,0:T(1,128)S(1)} async-done(((f32[128,1,737]{2,1,0:T(1,128)}), f32[128,1,737]{2,1,0:T(1,128)S(1)}, u32[]{:S(2)}, u32[]{:S(2)}) %all-to-all-start) | async-done | bytes 377376 | tf_op jit(solution)/shard_map/all_to_all | solution.py:132
  65.7 0.7 reduce.17
  66.6 0.9 reshape.199
  67.4 5.6 %all-to-all-start.1 = ((bf16[128,2,368]{2,1,0:T(2,128)(2,1)}), bf16[128,2,368]{2,1,0:T(2,128)(2,1)S(1)}, u32[]{:S(2)}, u32[]{:S(2)}) async-start(bf16[128,2,368]{2,1,0:T(2,128)(2,1)} %reshape.199), calls=%async_computation.1 | async-start | bytes 393216 | tf_op jit(solution)/shard_map/all_to_all | solution.py:151
  73.8 3.5 %multiply_subtract_fusion = (f32[1,1,94208]{2,1,0:T(1,128)}, f32[1,1,94208]{2,1,0:T(1,128)}, f32[1,1,94208]{2,1,0:T(1,128)}) fusion(f32[1,1,94208]{2,1,0:T(1,128)S(1)} %copy-done, f32[1,1,94208]{2,1,0:T(1,128)S(1)} %mul.192, f32[1,1,94208]{2,1,0:T(1,128)S(1)} %copy-done.2, f32[1,1,94208]{2,1,0:T(1,128)S(1)} %copy-done.1), kind=kLoop, calls=%fused_computation.12 | loop fusion | flops 1413120 | bytes 2637824 | tf_op jit(solution)/shard_map/sub | solution.py:30
  78.6 8.5 %all-to-all-done.1 = bf16[128,2,368]{2,1,0:T(2,128)(2,1)S(1)} async-done(((bf16[128,2,368]{2,1,0:T(2,128)(2,1)}), bf16[128,2,368]{2,1,0:T(2,128)(2,1)S(1)}, u32[]{:S(2)}, u32[]{:S(2)}) %all-to-all-start.1) | async-done | bytes 188448 | tf_op jit(solution)/shard_map/all_to_all | solution.py:151
  88.6 1.3 %reshape.170 = bf16[16,1280]{1,0:T(8,128)(2,1)} reshape(bf16[16,128,10]{2,1,0:T(8,128)(2,1)S(1)} %copy.105) | data formatting | bytes 81920 | tf_op jit(solution)/shard_map/reshape | solution.py:157
  90.2 1.3 %reshape.171 = bf16[16,1280]{1,0:T(8,128)(2,1)} reshape(bf16[16,128,10]{2,1,0:T(8,128)(2,1)S(1)} %copy.106) | data formatting | bytes 81920 | tf_op jit(solution)/shard_map/reshape | solution.py:157
  91.8 1.3 %reshape.172 = bf16[16,1280]{1,0:T(8,128)(2,1)} reshape(bf16[16,128,10]{2,1,0:T(8,128)(2,1)S(1)} %copy.107) | data formatting | bytes 81920 | tf_op jit(solution)/shard_map/reshape | solution.py:157
  93.2 0.7 copy.108
  94.0 0.7 copy.109
  94.9 0.7 copy.110
  95.7 0.7 copy.111
  (78 shorter events, 12.2 us)
Async XLA Ops:
  3.4 10.9 %copy-start.9 = (f32[16,512]{1,0:T(8,128)S(1)}, f32[16,512]{1,0:T(8,128)}, u32[]{:S(2)}) copy-start(f32[16,512]{1,0:T(8,128)} %get-tuple-element.23) | copy-start | bytes 98308
  4.1 19.6 %collective-permute-start = (f32[160]{0:T(256)S(1)}, f32[160]{0:T(256)S(1)}, u32[]{:S(2)}, u32[]{:S(2)}) collective-permute-start(f32[160]{0:T(256)S(1)} %pad_maximum_fusion), channel_id=1, source_target_pairs={{0,3},{1,0},{2,1},{3,2},{4,7},{5,4},{6,5},{7,6},{8,11},{9,8},{10,9... | collective-permute-start | bytes 1928 | tf_op jit(solution)/shard_map/ppermute | solution.py:86
  9.3 14.4 %collective-permute-start.1 = (f32[160]{0:T(256)S(1)}, f32[160]{0:T(256)S(1)}, u32[]{:S(2)}, u32[]{:S(2)}) collective-permute-start(f32[160]{0:T(256)S(1)} %pad_maximum_fusion), channel_id=1, source_target_pairs={{0,2},{1,3},{2,0},{3,1},{4,6},{5,7},{6,4},{7,5},{8,10},{9,11},{10,... | collective-permute-start | bytes 1928 | tf_op jit(solution)/shard_map/ppermute | solution.py:86
  11.8 11.9 %collective-permute-start.2 = (f32[160]{0:T(256)S(1)}, f32[160]{0:T(256)S(1)}, u32[]{:S(2)}, u32[]{:S(2)}) collective-permute-start(f32[160]{0:T(256)S(1)} %pad_maximum_fusion), channel_id=1, source_target_pairs={{0,1},{1,2},{2,3},{3,0},{4,5},{5,6},{6,7},{7,4},{8,9},{9,10},{10,1... | collective-permute-start | bytes 1928 | tf_op jit(solution)/shard_map/ppermute | solution.py:86
  14.5 0.8 copy-start.8
  15.5 0.8 copy-start.7
  16.4 0.8 copy-start.6
  17.2 0.9 copy-start.5
  19.2 0.9 copy-start.4
  21.1 0.9 copy-start.3
  26.4 18.6 %copy-start.1 = (f32[1,1,94208]{2,1,0:T(1,128)S(1)}, f32[1,1,94208]{2,1,0:T(1,128)}, u32[]{:S(2)}) copy-start(f32[1,1,94208]{2,1,0:T(1,128)} %param.24) | copy-start | bytes 1130500
  26.4 18.6 %copy-start.2 = (f32[1,1,94208]{2,1,0:T(1,128)S(1)}, f32[1,1,94208]{2,1,0:T(1,128)}, u32[]{:S(2)}) copy-start(f32[1,1,94208]{2,1,0:T(1,128)} %param.23) | copy-start | bytes 1130500
  26.4 36.4 %all-to-all-start = ((f32[128,1,737]{2,1,0:T(1,128)}), f32[128,1,737]{2,1,0:T(1,128)S(1)}, u32[]{:S(2)}, u32[]{:S(2)}) async-start(f32[128,1,737]{2,1,0:T(1,128)} %copy.92), calls=%async_computation | async-start | bytes 786432 | tf_op jit(solution)/shard_map/all_to_all | solution.py:132
  48.0 1.0 %copy-start = (f32[1,1,94208]{2,1,0:T(1,128)S(1)}, f32[1,1,94208]{2,1,0:T(1,128)}, u32[]{:S(2)}) copy-start(f32[1,1,94208]{2,1,0:T(1,128)} %param.22) | copy-start | bytes 1130500
  67.4 19.7 %all-to-all-start.1 = ((bf16[128,2,368]{2,1,0:T(2,128)(2,1)}), bf16[128,2,368]{2,1,0:T(2,128)(2,1)S(1)}, u32[]{:S(2)}, u32[]{:S(2)}) async-start(bf16[128,2,368]{2,1,0:T(2,128)(2,1)} %reshape.199), calls=%async_computation.1 | async-start | bytes 393216 | tf_op jit(solution)/shard_map/all_to_all | solution.py:151
  73.8 3.6 %copy-start.11 = (f32[2,16]{1,0:T(2,128)S(1)}, f32[2,16]{1,0:T(2,128)}, u32[]{:S(2)}) copy-start(f32[2,16]{1,0:T(2,128)} %param.26) | copy-start | bytes 388
  73.8 3.6 %copy-start.12 = (f32[2,16]{1,0:T(2,128)S(1)}, f32[2,16]{1,0:T(2,128)}, u32[]{:S(2)}) copy-start(f32[2,16]{1,0:T(2,128)} %param.27) | copy-start | bytes 388
  77.4 0.7 copy-start.10

commit v6 on v2

--- a/solution.py
+++ b/solution.py
@@ -114,7 +114,7 @@
         gain_master, gain_grad, gain_first, gain_second, 0.0, factor
     )
 
-    lowered = weights.astype(jnp.bfloat16).reshape(shard_count, rows * flat_width)
+    lowered = weights.astype(jnp.bfloat16)
     returned = lax.all_to_all(lowered, "shard", split_axis=0, concat_axis=0, tiled=True)
     returned = returned.reshape(shard_count, rows, flat_width)
     copies = []

time: 97.8 us -> 99.3 us (1.015)
  other arithmetic: 11.7 us -> 12.8 us
    unnamed x1 -> x2, other arithmetic: 1.53 us -> 3.39 us
    all_to_all x2 -> x0, other arithmetic: 1.04 us -> none  [shards(): lax.all_to_all(lowered, 'shard', split_axis=0, concat_axis=0, tiled=True)]
where the time goes in v6:
time: 99.3 us; the launch traced here: 98.6 us
  starting transfers between devices  32.3 us (33%)
  local copies, waits for them, and re-layouts  28.5 us (29%)
  waiting for transfers between devices  22 us (22%)
  other arithmetic  12.8 us (13%)
  between operations  3.08 us (3%)
    all_to_all x1, starting transfers between devices, shards(): lax.all_to_all(payload, 'shard', split_axis=0, concat_axis=0, tiled=True)  19.2 us
    all_to_all x1, waiting for transfers between devices, shards(): lax.all_to_all(payload, 'shard', split_axis=0, concat_axis=0, tiled=True)  11.9 us
    unnamed x40, local copies, waits for them, and re-layouts  11.5 us
    all_to_all x1, waiting for transfers between devices, shards(): lax.all_to_all(lowered, 'shard', split_axis=0, concat_axis=0, tiled=True)  8.45 us
    ppermute x2, starting transfers between devices, tensor_sum(): value = value + lax.ppermute(value, 'tensor', pairs)  7.64 us
    all_to_all x1, starting transfers between devices, shards(): lax.all_to_all(lowered, 'shard', split_axis=0, concat_axis=0, tiled=True)  5.53 us
    mul x14, local copies, waits for them, and re-layouts, mean_block(): return jnp.sum(matrix.astype(jnp.float32), axis=0) * (1.0 / MB)  5.1 us
    reshape x3, local copies, waits for them, and re-layouts, shards(): jnp.transpose(section, (1, 0, 2)).reshape(rows, shard_count * group_width)  3.86 us
  transfers between devices with their start and end apart: 4, of which 3 were waited for; matrix products, arithmetic and copies ran while one was open for 16% of the time, Pallas kernels for 0%

profile of v6, /device:TPU:1, one launch (start us, length us, event | category | flops | bytes accessed | tf_op | source)
XLA Modules:
  0.0 98.6 jit_solution(4736902498192790715)
XLA Ops:
  0.6 0.9 convert_reduce_fusion.2
  1.6 0.9 copy-done.3
  2.7 0.8 copy-done.4
  3.6 0.8 copy-done.5
  4.5 0.8 copy-done.6
  5.3 0.8 copy-done.7
  6.2 0.8 copy-done.8
  7.9 3.9 %collective-permute-start = (f32[160]{0:T(256)S(1)}, f32[160]{0:T(256)S(1)}, u32[]{:S(2)}, u32[]{:S(2)}) collective-permute-start(f32[160]{0:T(256)S(1)} %pad_maximum_fusion), channel_id=1, source_target_pairs={{0,1},{1,0},{2,3},{3,2},{4,5},{5,4},{6,7},{7,6},{8,9},{9,8},{10,11... | collective-permute-start | bytes 1928 | tf_op jit(solution)/shard_map/ppermute | solution.py:54
  12.8 1.1 %mul.314 = f32[16,128,10]{2,1,0:T(8,128)S(1)} reshape(f32[16,1280]{1,0:T(8,128)S(1)} %get-tuple-element.92) | data formatting | bytes 163840 | tf_op jit(solution)/shard_map/mul | solution.py:32
  14.2 1.1 %mul.316 = f32[16,128,10]{2,1,0:T(8,128)S(1)} reshape(f32[16,1280]{1,0:T(8,128)S(1)} %get-tuple-element.94) | data formatting | bytes 163840 | tf_op jit(solution)/shard_map/mul | solution.py:32
  15.7 1.1 %mul.318 = f32[16,128,10]{2,1,0:T(8,128)S(1)} reshape(f32[16,1280]{1,0:T(8,128)S(1)} %get-tuple-element.96) | data formatting | bytes 163840 | tf_op jit(solution)/shard_map/mul | solution.py:32
  17.2 3.7 %collective-permute-start.1 = (f32[160]{0:T(256)S(1)}, f32[160]{0:T(256)S(1)}, u32[]{:S(2)}, u32[]{:S(2)}) collective-permute-start(f32[160]{0:T(256)S(1)} %fusion.9), channel_id=1, source_target_pairs={{0,3},{1,2},{2,1},{3,0},{4,7},{5,6},{6,5},{7,4},{8,11},{9,10},{10,... | collective-permute-start | bytes 1928 | tf_op jit(solution)/shard_map/ppermute | solution.py:54
  21.1 1.6 %collective-permute-done.1 = f32[160]{0:T(256)S(1)} collective-permute-done((f32[160]{0:T(256)S(1)}, f32[160]{0:T(256)S(1)}, u32[]{:S(2)}, u32[]{:S(2)}) %collective-permute-start.1) | collective-permute-done | bytes 672 | tf_op jit(solution)/shard_map/ppermute | solution.py:54
  22.7 0.7 add_reduce_fusion
  24.1 1.3 %copy.113 = f32[128,1,737]{2,1,0:T(1,128)} copy(f32[128,1,737]{0,2,1:T(8,128)S(1)} %pad_bitcast_fusion) | data formatting | bytes 754688 | tf_op jit(solution)/shard_map/all_to_all | solution.py:99
  25.4 19.2 %all-to-all-start = ((f32[128,1,737]{2,1,0:T(1,128)}), f32[128,1,737]{2,1,0:T(1,128)S(1)}, u32[]{:S(2)}, u32[]{:S(2)}) async-start(f32[128,1,737]{2,1,0:T(1,128)} %copy.113), calls=%async_computation | async-start | bytes 786432 | tf_op jit(solution)/shard_map/all_to_all | solution.py:99
  44.6 2.3 %multiply_reduce_fusion = (f32[94208]{0:T(1024)S(1)}, f32[94208]{0:T(1024)S(1)}) fusion(f32[1,1,94208]{2,1,0:T(1,128)S(1)} %copy-done.1, f32[1,1,94208]{2,1,0:T(1,128)S(1)} %copy-done.2), kind=kLoop, calls=%fused_computation.17 | loop fusion | flops 188416 | bytes 1507328 | tf_op jit(solution)/shard_map/mul | solution.py:22
  48.5 1.5 %reduce.12 = f32[94208]{0:T(1024)S(1)} reduce(f32[1,1,94208]{2,1,0:T(1,128)S(1)} %copy-done, f32[]{:T(128)} %broadcast.146), dimensions={0,1}, to_apply=%param.22.reduce_sub_computation.3 | reduce | bytes 753668 | tf_op args[8]
  50.5 11.9 %all-to-all-done = f32[128,1,737]{2,1,0:T(1,128)S(1)} async-done(((f32[128,1,737]{2,1,0:T(1,128)}), f32[128,1,737]{2,1,0:T(1,128)S(1)}, u32[]{:S(2)}, u32[]{:S(2)}) %all-to-all-start) | async-done | bytes 377376 | tf_op jit(solution)/shard_map/all_to_all | solution.py:99
  64.7 0.7 copy.120
  65.9 1.9 %reduce.13 = bf16[128,736]{1,0:T(8,128)(2,1)S(1)} reduce(bf16[128,1,736]{2,1,0:T(2,128)(2,1)S(1)} %bitcast.35, bf16[]{:T(256)} %broadcast.147), dimensions={1}, to_apply=%bitcast.32.reduce_sub_computation | reduce | bytes 376834
  67.8 0.9 reshape.239
  68.7 5.5 %all-to-all-start.1 = ((bf16[128,2,368]{2,1,0:T(2,128)(2,1)}), bf16[128,2,368]{2,1,0:T(2,128)(2,1)S(1)}, u32[]{:S(2)}, u32[]{:S(2)}) async-start(bf16[128,2,368]{2,1,0:T(2,128)(2,1)} %reshape.239), calls=%async_computation.1 | async-start | bytes 393216 | tf_op jit(solution)/shard_map/all_to_all | solution.py:118
  75.0 3.5 %multiply_subtract_fusion = (f32[1,1,94208]{2,1,0:T(1,128)}, f32[1,1,94208]{2,1,0:T(1,128)}, f32[1,1,94208]{2,1,0:T(1,128)}) fusion(f32[1,1,94208]{2,1,0:T(1,128)S(1)} %copy-done, f32[1,1,94208]{2,1,0:T(1,128)S(1)} %mul.338, f32[1,1,94208]{2,1,0:T(1,128)S(1)} %copy-done.2, f32[1,1,94208]{2,1,0:T(1,128)S(1)} %copy-done.1), kind=kLoop, calls=%fused_computation.12 | loop fusion | flops 1413120 | bytes 2637824 | tf_op jit(solution)/shard_map/sub | solution.py:28
  79.8 8.4 %all-to-all-done.1 = bf16[128,2,368]{2,1,0:T(2,128)(2,1)S(1)} async-done(((bf16[128,2,368]{2,1,0:T(2,128)(2,1)}), bf16[128,2,368]{2,1,0:T(2,128)(2,1)S(1)}, u32[]{:S(2)}, u32[]{:S(2)}) %all-to-all-start.1) | async-done | bytes 188448 | tf_op jit(solution)/shard_map/all_to_all | solution.py:118
  89.7 1.3 %reshape.217 = bf16[16,1280]{1,0:T(8,128)(2,1)} reshape(bf16[16,128,10]{2,1,0:T(8,128)(2,1)S(1)} %copy.126) | data formatting | bytes 81920 | tf_op jit(solution)/shard_map/reshape | solution.py:124
  91.3 1.3 %reshape.218 = bf16[16,1280]{1,0:T(8,128)(2,1)} reshape(bf16[16,128,10]{2,1,0:T(8,128)(2,1)S(1)} %copy.127) | data formatting | bytes 81920 | tf_op jit(solution)/shard_map/reshape | solution.py:124
  92.9 1.3 %reshape.219 = bf16[16,1280]{1,0:T(8,128)(2,1)} reshape(bf16[16,128,10]{2,1,0:T(8,128)(2,1)S(1)} %copy.128) | data formatting | bytes 81920 | tf_op jit(solution)/shard_map/reshape | solution.py:124
  94.3 0.7 copy.129
  95.1 0.7 copy.130
  96.0 0.7 copy.131
  96.8 0.7 copy.132
  (104 shorter events, 13.0 us)
Async XLA Ops:
  1.6 0.9 copy-start.3
  2.6 0.9 copy-start.4
  3.5 0.8 copy-start.5
  4.4 0.8 copy-start.6
  5.3 0.8 copy-start.7
  6.2 0.8 copy-start.8
  7.0 0.7 copy-start.9
  7.9 9.2 %collective-permute-start = (f32[160]{0:T(256)S(1)}, f32[160]{0:T(256)S(1)}, u32[]{:S(2)}, u32[]{:S(2)}) collective-permute-start(f32[160]{0:T(256)S(1)} %pad_maximum_fusion), channel_id=1, source_target_pairs={{0,1},{1,0},{2,3},{3,2},{4,5},{5,4},{6,7},{7,6},{8,9},{9,8},{10,11... | collective-permute-start | bytes 1928 | tf_op jit(solution)/shard_map/ppermute | solution.py:54
  17.2 5.5 %collective-permute-start.1 = (f32[160]{0:T(256)S(1)}, f32[160]{0:T(256)S(1)}, u32[]{:S(2)}, u32[]{:S(2)}) collective-permute-start(f32[160]{0:T(256)S(1)} %fusion.9), channel_id=1, source_target_pairs={{0,3},{1,2},{2,1},{3,0},{4,7},{5,6},{6,5},{7,4},{8,11},{9,10},{10,... | collective-permute-start | bytes 1928 | tf_op jit(solution)/shard_map/ppermute | solution.py:54
  25.4 19.2 %copy-start.1 = (f32[1,1,94208]{2,1,0:T(1,128)S(1)}, f32[1,1,94208]{2,1,0:T(1,128)}, u32[]{:S(2)}) copy-start(f32[1,1,94208]{2,1,0:T(1,128)} %param.24) | copy-start | bytes 1130500
  25.4 19.2 %copy-start.2 = (f32[1,1,94208]{2,1,0:T(1,128)S(1)}, f32[1,1,94208]{2,1,0:T(1,128)}, u32[]{:S(2)}) copy-start(f32[1,1,94208]{2,1,0:T(1,128)} %param.23) | copy-start | bytes 1130500
  25.4 37.0 %all-to-all-start = ((f32[128,1,737]{2,1,0:T(1,128)}), f32[128,1,737]{2,1,0:T(1,128)S(1)}, u32[]{:S(2)}, u32[]{:S(2)}) async-start(f32[128,1,737]{2,1,0:T(1,128)} %copy.113), calls=%async_computation | async-start | bytes 786432 | tf_op jit(solution)/shard_map/all_to_all | solution.py:99
  47.5 1.0 %copy-start = (f32[1,1,94208]{2,1,0:T(1,128)S(1)}, f32[1,1,94208]{2,1,0:T(1,128)}, u32[]{:S(2)}) copy-start(f32[1,1,94208]{2,1,0:T(1,128)} %param.22) | copy-start | bytes 1130500
  68.7 19.5 %all-to-all-start.1 = ((bf16[128,2,368]{2,1,0:T(2,128)(2,1)}), bf16[128,2,368]{2,1,0:T(2,128)(2,1)S(1)}, u32[]{:S(2)}, u32[]{:S(2)}) async-start(bf16[128,2,368]{2,1,0:T(2,128)(2,1)} %reshape.239), calls=%async_computation.1 | async-start | bytes 393216 | tf_op jit(solution)/shard_map/all_to_all | solution.py:118
  75.0 3.6 %copy-start.11 = (f32[2,16]{1,0:T(2,128)S(1)}, f32[2,16]{1,0:T(2,128)}, u32[]{:S(2)}) copy-start(f32[2,16]{1,0:T(2,128)} %param.26) | copy-start | bytes 388
  75.0 3.6 %copy-start.12 = (f32[2,16]{1,0:T(2,128)S(1)}, f32[2,16]{1,0:T(2,128)}, u32[]{:S(2)}) copy-start(f32[2,16]{1,0:T(2,128)} %param.27) | copy-start | bytes 388
  78.5 0.7 copy-start.10
